TPU v7x, 512 devices: a whole 4x4x16 slice. The times are simulated.
512 devices in a mesh: dp: 8 (over z_hi, core), seq: 64 (over z_lo, y, x).
Axes of the slice: x: 4, y: 4, z: 16 (z_hi: 4, z_lo: 4; z = z_hi * 4 + z_lo), core: 2. Of those that a mesh axis runs over, the one named last changes fastest.
Arguments:
- query: bfloat16 [8, 8192, 512], P('dp', 'seq'), may hold values from -6 to 6
- key_in: bfloat16 [8, 8192, 128], P('dp', 'seq'), may hold values from -4.5 to 4.5
- value_in: bfloat16 [8, 8192, 128], P('dp', 'seq'), may hold values from -6 to 6
- out_gain: float32 [512], replicated, may hold values from 0.1 to 1.9
- cotangent: bfloat16 [8, 8192, 512], P('dp', 'seq'), may hold values from -6 to 6
Outputs:
- attended: bfloat16 [8, 8192, 512], P('dp', 'seq')
- grad_query: bfloat16 [8, 8192, 512], P('dp', 'seq')
- grad_key: bfloat16 [8, 8192, 128], P('dp', 'seq')
- grad_value: bfloat16 [8, 8192, 128], P('dp', 'seq')
- grad_gain: float32 [512], replicated
All inputs are finite; a program needn't handle non-finite values.
Results may differ from a plain program's by a relative error of at most 0.012.
The roundings to bfloat16 on the way count: a program that leaves them out, or rounds other values in their place, can miss the bound.
Values may be sent and summed in bfloat16 or wider, within the bound.
No kernel may reach another device: no remote copies, remote signals or barrier semaphores. Data moves between devices by JAX's collectives and lax.ppermute only.
A program may use at most 128 MiB of HBM per device.

v0:
```python
import math

import jax
import jax.numpy as jnp
from jax import lax
from jax.sharding import PartitionSpec as P

HEADS = 4
KEY = 128
VAL = 128


def to_rows(tokens, heads):
    positions = tokens.shape[0]
    width = tokens.shape[1] // heads
    return (
        tokens.reshape(positions, heads, width).transpose(1, 0, 2).reshape(heads * positions, width)
    )


def to_tokens(rows_in, heads):
    positions = rows_in.shape[0] // heads
    width = rows_in.shape[1]
    return (
        rows_in.reshape(heads, positions, width)
        .transpose(1, 0, 2)
        .reshape(positions, heads * width)
    )


def contract_first(left_mat, right_mat):
    return lax.dot_general(
        left_mat, right_mat, (((0,), (0,)), ((), ())), preferred_element_type=jnp.float32
    )


def contract_last(left_mat, right_mat):
    return lax.dot_general(
        left_mat, right_mat, (((1,), (1,)), ((), ())), preferred_element_type=jnp.float32
    )


def body(query, key_in, value_in, out_gain, cotangent):
    keys_all, values_all = (
        lax.all_gather(key_in, "seq", axis=1, tiled=True),
        lax.all_gather(value_in, "seq", axis=1, tiled=True),
    )
    key_mat = keys_all[0]
    value_mat = values_all[0]
    length = key_mat.shape[0]
    positions = query.shape[1]
    shards = lax.axis_size("seq")
    score_scale = 1.0 / math.sqrt(KEY)
    query_rows = to_rows(query[0], HEADS)
    scores = contract_last(query_rows, key_mat) * score_scale
    row_top = jnp.max(scores, axis=1, keepdims=True)
    expo_rows = jnp.exp(scores - row_top)
    weights = (expo_rows / jnp.sum(expo_rows, axis=1, keepdims=True)).astype(jnp.bfloat16)
    out_rows = jnp.dot(weights, value_mat, preferred_element_type=jnp.float32)
    out_tokens = to_tokens(out_rows, HEADS)
    attended = (out_tokens * out_gain).astype(jnp.bfloat16)
    upstream = cotangent[0].astype(jnp.float32)
    gain_total = lax.psum(jnp.sum(upstream * out_tokens, axis=0), ("dp", "seq"))
    token_total = lax.axis_size("dp") * shards * positions
    grad_gain = gain_total / math.sqrt(token_total)
    grad_out = (upstream * out_gain).astype(jnp.bfloat16)
    grad_rows = to_rows(grad_out, HEADS)
    delta_rows = jnp.sum(grad_rows.astype(jnp.float32) * out_rows, axis=1, keepdims=True)
    block_size = 2048
    block_starts = jnp.arange(length // block_size, dtype=jnp.int32) * block_size
    query_zero = jnp.zeros((query_rows.shape[0], KEY), jnp.float32)

    def score_grad(offset_at):
        key_part = lax.dynamic_slice_in_dim(key_mat, offset_at, block_size, 0)
        value_part = lax.dynamic_slice_in_dim(value_mat, offset_at, block_size, 0)
        weight_part = lax.dynamic_slice_in_dim(weights, offset_at, block_size, 1)
        d_prob = contract_last(grad_rows, value_part)
        d_score = (weight_part.astype(jnp.float32) * (d_prob - delta_rows)).astype(jnp.bfloat16)
        return (d_score, key_part, weight_part)

    def advance_both(query_acc, offset_at):
        d_score, key_part, weight_part = score_grad(offset_at)
        query_acc = query_acc + jnp.dot(d_score, key_part, preferred_element_type=jnp.float32)
        key_term = contract_first(d_score, query_rows) * score_scale
        value_term = contract_first(weight_part, grad_rows)
        return (query_acc, (key_term, value_term))

    query_acc, both_terms = lax.scan(advance_both, query_zero, block_starts)
    key_recv, value_recv = (
        lax.all_to_all(
            both_terms[0].reshape(shards, positions, KEY),
            "seq",
            split_axis=0,
            concat_axis=0,
            tiled=True,
        ),
        lax.all_to_all(
            both_terms[1].reshape(shards, positions, VAL),
            "seq",
            split_axis=0,
            concat_axis=0,
            tiled=True,
        ),
    )
    grad_key = jnp.sum(key_recv, axis=0)
    grad_value = jnp.sum(value_recv, axis=0)
    grad_query = to_tokens(query_acc * score_scale, HEADS).astype(jnp.bfloat16)
    return (
        attended[None],
        grad_query[None],
        grad_key.astype(jnp.bfloat16)[None],
        grad_value.astype(jnp.bfloat16)[None],
        grad_gain,
    )


def solution(mesh):
    placed = (
        P("dp", "seq", None),
        P("dp", "seq", None),
        P("dp", "seq", None),
        P(),
        P("dp", "seq", None),
    )
    return jax.shard_map(
        body,
        mesh=mesh,
        in_specs=placed,
        out_specs=(
            P("dp", "seq", None),
            P("dp", "seq", None),
            P("dp", "seq", None),
            P("dp", "seq", None),
            P(),
        ),
        check_vma=False,
    )
```

profile of v0, /device:TPU:1, one launch (start us, length us, event | category | flops | bytes accessed | tf_op | source)
XLA Modules:
  0.0 1053.3 jit_solution(2763086969932441278)
XLA Ops:
  10.7 312.2 %all-gather.3.cloned.1.call-done = bf16[1,8192,128]{2,1,0:T(8,128)(2,1)} async-done(((bf16[1,128,128]{2,1,0:T(8,128)(2,1)}), bf16[1,8192,128]{2,1,0:T(8,128)(2,1)}) %all-gather.3.cloned.1.call-update) | async-done | bytes 2097168 | tf_op jit(solution)/shard_map/all_gather | solution.py:45
  322.9 9.6 multiply_reduce_fusion
  332.5 8.6 fusion.8
  341.1 10.3 divide_convert_fusion
  351.5 326.2 %all-gather.5.cloned.1.call-done = bf16[1,8192,128]{2,1,0:T(8,128)(2,1)} async-done(((bf16[1,128,128]{2,1,0:T(8,128)(2,1)}), bf16[1,8192,128]{2,1,0:T(8,128)(2,1)}) %all-gather.5.cloned.1.call-update) | async-done | bytes 2097168 | tf_op jit(solution)/shard_map/all_gather | solution.py:46
  677.7 6.3 multiply_reduce_fusion.1
  684.2 77.3 %while.15 = (s32[]{:T(128)}, f32[512,128]{1,0:T(8,128)S(1)}, f32[4,2048,128]{2,1,0:T(8,128)}, f32[4,2048,128]{2,1,0:T(8,128)}, s32[4]{0:T(128)S(1)}, /*index=5*/...) while((s32[]{:T(128)}, f32[512,128]{1,0:T(8,128)S(1)}, ...), condition=%wide.region_4.0_spmd.clone, body=%wide.region_3.0_spmd.clone.sunk | while | flops 1078329344 | bytes 22939864 | solution.py:88
  686.7 2.9 constant_dynamic-slice_fusion.2
  689.6 2.5 copy.22
  692.1 3.9 fusion.40
  696.0 2.4 convolution_add_fusion.2
  698.5 3.4 fusion.41
  706.2 2.9 constant_dynamic-slice_fusion.2
  709.1 2.5 copy.22
  711.6 3.9 fusion.40
  715.5 2.5 convolution_add_fusion.2
  717.9 3.3 fusion.41
  725.4 2.9 constant_dynamic-slice_fusion.2
  728.3 2.5 copy.22
  730.9 3.9 fusion.40
  734.8 2.5 convolution_add_fusion.2
  737.2 3.3 fusion.41
  744.7 2.9 constant_dynamic-slice_fusion.2
  747.6 2.5 copy.22
  750.1 3.9 fusion.40
  754.0 2.5 convolution_add_fusion.2
  756.5 3.3 fusion.41
  761.5 60.0 %all_to_all.10 = f32[64,128,128]{2,1,0:T(8,128)} all-to-all(f32[64,128,128]{2,1,0:T(8,128)} %bitcast.85), channel_id=1, replica_groups=mesh['dp'=8,'seq'=64] {'seq'}, dimensions={0} | all-to-all | bytes 8388608 | tf_op jit(solution)/shard_map/all_to_all | solution.py:90
  821.4 5.7 all-to-all-start.1
  828.3 210.9 %psum.7 = f32[512]{0:T(512)S(1)} all-reduce(f32[512]{0:T(512)S(1)} %bitcast.95), channel_id=1, replica_groups=mesh['dp'=8,'seq'=64] {'dp','seq'}, use_global_device_ids=true, to_apply=%region_8.9 | all-reduce | flops 512 | bytes 4096 | tf_op jit(solution)/shard_map/psum | solution.py:63
  1040.4 3.0 reduce_sum.49
  1043.5 3.0 reduce_sum.50
  (30 shorter events, 15.2 us)
Async XLA Ops:
  7.2 315.7 %all-gather.3.cloned.1.call-start = ((), (), s32[]{:S(2)}) async-start(), calls=%async_computation.2 | async-start | bytes 2129920 | tf_op jit(solution)/shard_map/all_gather | solution.py:45
  7.9 669.8 %all-gather.5.cloned.1.call-start = ((), (), s32[]{:S(2)}) async-start(), calls=%async_computation.3 | async-start | bytes 2129920 | tf_op jit(solution)/shard_map/all_gather | solution.py:46
  341.1 336.5 %copy-start = (f32[512]{0:T(512)S(1)}, f32[512]{0:T(512)}, u32[]{:S(2)}) copy-start(f32[512]{0:T(512)} %param.10) | copy-start | bytes 6148
  821.4 222.0 %all-to-all-start.1 = ((f32[64,128,128]{2,1,0:T(8,128)}), f32[64,128,128]{2,1,0:T(8,128)}, u32[]{:S(2)}, u32[]{:S(2)}) async-start(f32[64,128,128]{2,1,0:T(8,128)} %bitcast.86), calls=%async_computation.1 | async-start | bytes 8388608 | tf_op jit(solution)/shard_map/all_to_all | solution.py:97
Sparse Core Ops, SparseCore 0:
  10.1 312.7 all-gather.2
  324.9 352.6 all-gather.4
where the time goes:
time: 1050 us
  waiting for transfers between devices  640 us (61%)
  blocking collectives  271 us (26%)
  matrix products  61.4 us (6%)
  local copies, waits for them, and re-layouts  27.1 us (3%)
  other arithmetic  26.4 us (3%)
  between operations  14.1 us (1%)
    all_gather x1, waiting for transfers between devices, body(): lax.all_gather(value_in, 'seq', axis=1, tiled=True)  326 us
    all_gather x1, waiting for transfers between devices, body(): lax.all_gather(key_in, 'seq', axis=1, tiled=True)  312 us
    psum x1, blocking collectives, body(): gain_total = lax.psum(jnp.sum(upstream * out_tokens, axis=0), ('dp', 'seq'))  211 us
    all_to_all x1, blocking collectives, body(): lax.all_to_all(both_terms[0].reshape(shards, positions, KEY), 'seq', spli...  60 us
    dot_general x5, matrix products, contract_last(): lax.dot_general(left_mat, right_mat, (((1,), (1,)), ((), ())), preferred_...  25.2 us
    dynamic_slice x8, local copies, waits for them, and re-layouts, score_grad(): weight_part = lax.dynamic_slice_in_dim(weights, offset_at, block_size, 1)  21.7 us
  transfers between devices with their start and end apart: 3, of which 2 were waited for; matrix products, arithmetic and copies ran while one was open for 3% of the time, Pallas kernels for 0%

commit v1 on v0

--- a/solution.py
+++ b/solution.py
@@ -41,15 +41,19 @@
 
 
 def body(query, key_in, value_in, out_gain, cotangent):
-    keys_all, values_all = (
-        lax.all_gather(key_in, "seq", axis=1, tiled=True),
-        lax.all_gather(value_in, "seq", axis=1, tiled=True),
-    )
-    key_mat = keys_all[0]
-    value_mat = values_all[0]
-    length = key_mat.shape[0]
     positions = query.shape[1]
     shards = lax.axis_size("seq")
+    local_kv = jnp.concatenate([key_in[0], value_in[0]], axis=1)
+    kv_all = lax.all_to_all(
+        jnp.broadcast_to(local_kv[None], (shards,) + local_kv.shape),
+        "seq",
+        split_axis=0,
+        concat_axis=0,
+        tiled=True,
+    ).reshape(shards * positions, KEY + VAL)
+    key_mat = kv_all[:, :KEY]
+    value_mat = kv_all[:, KEY:]
+    length = key_mat.shape[0]
     score_scale = 1.0 / math.sqrt(KEY)
     query_rows = to_rows(query[0], HEADS)
     scores = contract_last(query_rows, key_mat) * score_scale
@@ -60,9 +64,7 @@
     out_tokens = to_tokens(out_rows, HEADS)
     attended = (out_tokens * out_gain).astype(jnp.bfloat16)
     upstream = cotangent[0].astype(jnp.float32)
-    gain_total = lax.psum(jnp.sum(upstream * out_tokens, axis=0), ("dp", "seq"))
-    token_total = lax.axis_size("dp") * shards * positions
-    grad_gain = gain_total / math.sqrt(token_total)
+    gain_part = jnp.sum(upstream * out_tokens, axis=0)
     grad_out = (upstream * out_gain).astype(jnp.bfloat16)
     grad_rows = to_rows(grad_out, HEADS)
     delta_rows = jnp.sum(grad_rows.astype(jnp.float32) * out_rows, axis=1, keepdims=True)
@@ -86,24 +88,23 @@
         return (query_acc, (key_term, value_term))
 
     query_acc, both_terms = lax.scan(advance_both, query_zero, block_starts)
-    key_recv, value_recv = (
-        lax.all_to_all(
+    gain_rows = gain_part.reshape(HEADS, VAL)
+    payload = jnp.concatenate(
+        [
             both_terms[0].reshape(shards, positions, KEY),
-            "seq",
-            split_axis=0,
-            concat_axis=0,
-            tiled=True,
-        ),
-        lax.all_to_all(
             both_terms[1].reshape(shards, positions, VAL),
-            "seq",
-            split_axis=0,
-            concat_axis=0,
-            tiled=True,
-        ),
+            jnp.broadcast_to(gain_rows[None], (shards, HEADS, VAL)),
+        ],
+        axis=1,
     )
-    grad_key = jnp.sum(key_recv, axis=0)
-    grad_value = jnp.sum(value_recv, axis=0)
+    recv = jnp.sum(
+        lax.all_to_all(payload, "seq", split_axis=0, concat_axis=0, tiled=True), axis=0
+    )
+    grad_key = recv[:positions]
+    grad_value = recv[positions : 2 * positions]
+    gain_total = lax.psum(recv[2 * positions :].reshape(HEADS * VAL), "dp")
+    token_total = lax.axis_size("dp") * shards * positions
+    grad_gain = gain_total / math.sqrt(token_total)
     grad_query = to_tokens(query_acc * score_scale, HEADS).astype(jnp.bfloat16)
     return (
         attended[None],

time: 1050 us -> 435 us (0.41)
  waiting for transfers between devices: 640 us -> 283 us
  blocking collectives: 271 us -> 21.2 us
  starting transfers between devices: 5.74 us -> 20.5 us
  local copies, waits for them, and re-layouts: 27.1 us -> 13.6 us
  between operations: 14.1 us -> 0.78 us
    all_gather x2 -> x0, waiting for transfers between devices: 638 us -> none  [the longest x1 326 us: body(): lax.all_gather(value_in, 'seq', axis=1, tiled=True)]
    all_to_all x1 -> x2, waiting for transfers between devices: 0.01 us -> 283 us  [the longest x1 190 us: body(): lax.all_to_all(payload, 'seq', split_axis=0, concat_axis=0, tiled=True)]
    psum x1, blocking collectives: 211 us -> 21.2 us  [body(): gain_total = lax.psum(recv[2 * positions:].reshape(HEADS * VAL), 'dp')]
    all_to_all x1 -> x0, blocking collectives: 60 us -> none  [body(): lax.all_to_all(both_terms[0].reshape(shards, positions, KEY), 'seq', spli...]
    dynamic_slice x8 -> x0, local copies, waits for them, and re-layouts: 21.7 us -> none  [score_grad(): weight_part = lax.dynamic_slice_in_dim(weights, offset_at, block_size, 1)]
    all_to_all x1 -> x2, starting transfers between devices: 5.66 us -> 20.5 us  [the longest x1 12.9 us: body(): lax.all_to_all(jnp.broadcast_to(local_kv[None], (shards,) + local_kv.shap...]
    div x0 -> x1, other arithmetic: none -> 11.1 us  [body(): expo_rows / jnp.sum(expo_rows, axis=1, keepdims=True)]
  transfers between devices with their start and end apart: 3 -> 2, of which waited for: 2 -> 2; matrix products, arithmetic and copies ran while one was open for 3% -> 0% of each run, Pallas kernels for 0% -> 0%
where the time goes in v1:
time: 435 us; the launch traced here: 432 us
  waiting for transfers between devices  283 us (65%)
  matrix products  52.9 us (12%)
  other arithmetic  31.7 us (7%)
  blocking collectives  21.2 us (5%)
  starting transfers between devices  20.5 us (5%)
  local copies, waits for them, and re-layouts  13.6 us (3%)
  loops' own time  8.03 us (2%)
    all_to_all x1, waiting for transfers between devices, body(): lax.all_to_all(payload, 'seq', split_axis=0, concat_axis=0, tiled=True)  190 us
    all_to_all x1, waiting for transfers between devices, body(): lax.all_to_all(jnp.broadcast_to(local_kv[None], (shards,) + local_kv.shap...  93 us
    psum x1, blocking collectives, body(): gain_total = lax.psum(recv[2 * positions:].reshape(HEADS * VAL), 'dp')  21.2 us
    dot_general x5, matrix products, contract_last(): lax.dot_general(left_mat, right_mat, (((1,), (1,)), ((), ())), preferred_...  20.7 us
    dot_general x8, matrix products, contract_first(): lax.dot_general(left_mat, right_mat, (((0,), (0,)), ((), ())), preferred_...  20.1 us
    all_to_all x1, starting transfers between devices, body(): lax.all_to_all(jnp.broadcast_to(local_kv[None], (shards,) + local_kv.shap...  12.9 us
    div x1, other arithmetic, body(): expo_rows / jnp.sum(expo_rows, axis=1, keepdims=True)  11.1 us
  transfers between devices with their start and end apart: 2, of which 2 were waited for; matrix products, arithmetic and copies ran while one was open for 0% of the time, Pallas kernels for 0%

profile of v1, /device:TPU:1, one launch (start us, length us, event | category | flops | bytes accessed | tf_op | source)
XLA Modules:
  0.0 431.9 jit_solution(536330571685023800)
XLA Ops:
  0.6 0.8 pad_maximum_fusion.1
  1.4 2.4 broadcast_in_dim.36
  3.9 12.9 %all-to-all-start = ((bf16[64,128,256]{2,1,0:T(8,128)(2,1)}), bf16[64,128,256]{2,1,0:T(8,128)(2,1)}, u32[]{:S(2)}, u32[]{:S(2)}) async-start(bf16[64,128,256]{2,1,0:T(8,128)(2,1)} %broadcast_in_dim.36), calls=%async_computation | async-start | bytes 8388608 | tf_op jit(solution)/shard_map/all_to_all | solution.py:47
  17.0 93.0 %all-to-all-done = bf16[64,128,256]{2,1,0:T(8,128)(2,1)} async-done(((bf16[64,128,256]{2,1,0:T(8,128)(2,1)}), bf16[64,128,256]{2,1,0:T(8,128)(2,1)}, u32[]{:S(2)}, u32[]{:S(2)}) %all-to-all-start) | async-done | bytes 4194336 | tf_op jit(solution)/shard_map/all_to_all | solution.py:47
  110.0 4.4 %fusion.15 = (bf16[8192,128]{1,0:T(8,128)(2,1)}, bf16[8192,128]{1,0:T(8,128)(2,1)}) fusion(bf16[8192,256]{1,0:T(8,128)(2,1)} %bitcast.2), kind=kLoop, calls=%fused_computation.35 | loop fusion | bytes 8388608 | tf_op jit(solution)/shard_map/slice | solution.py:54
  114.4 9.6 %multiply_reduce_fusion = (f32[512]{0:T(512)S(1)}, f32[8192,512]{1,0:T(8,128)}) fusion(bf16[512,128]{1,0:T(8,128)(2,1)S(1)} %bitcast.72, bf16[8192,256]{1,0:T(8,128)(2,1)} %bitcast.2), kind=kOutput, calls=%fused_computation.16 | convolution fusion | flops 1082129920 | bytes 19007488 | tf_op jit(solution)/shard_map/dot_general | solution.py:38
  124.1 8.6 %fusion.10 = f32[512]{0:T(512)S(1)} fusion(f32[8192,512]{1,0:T(8,128)} %get-tuple-element.132, f32[512]{0:T(512)S(1)} %get-tuple-element.131), kind=kLoop, calls=%fused_computation.17 | loop fusion | flops 12582400 | bytes 16781312 | tf_op jit(solution)/shard_map/reduce_sum | solution.py:62
  132.7 11.1 %fusion.23 = bf16[512,8192]{0,1:T(8,128)(2,1)} fusion(f32[512]{0:T(512)S(1)} %fusion.10, f32[512]{0:T(512)S(1)} %get-tuple-element.131, f32[8192,512]{1,0:T(8,128)} %get-tuple-element.132), kind=kLoop, calls=%fused_computation.36 | loop fusion | flops 16777216 | bytes 25169920 | tf_op jit(solution)/shard_map/div | solution.py:62
  143.8 2.5 copy-done
  146.4 4.8 %multiply_reduce_fusion.1 = (f32[4,128]{1,0:T(4,128)S(1)}, bf16[128,4,128]{2,0,1:T(8,128)(2,1)S(1)}, f32[512,128]{1,0:T(8,128)S(1)}) fusion(f32[128,4,128]{2,1,0:T(4,128)S(1)} %reshape.106, f32[4,128]{1,0:T(4,128)S(1)} %bitcast.82, bf16[8192,256]{1,0:T(8,128)(2,1)} %bitcast.2, f32[8192,512]{1,0:T(8,128)S(1)} %copy-done, f32[512]{0:T(512)S(1)} %fusion.10, ...), kind=kOutput, calls=%fused_computation.19 | convolution fusion | flops 1090780672 | bytes 19537920 | tf_op jit(solution)/shard_map/dot_general | solution.py:63
  151.3 48.9 %while.15 = (s32[]{:T(128)}, f32[512,128]{1,0:T(8,128)S(1)}, f32[4,2048,128]{2,1,0:T(8,128)}, f32[4,2048,128]{2,1,0:T(8,128)}, s32[4]{0:T(128)S(1)}, /*index=5*/...) while((s32[]{:T(128)}, f32[512,128]{1,0:T(8,128)S(1)}, ...), condition=%wide.region_4.5_spmd.clone, body=%wide.region_3.0_spmd.clone.sunk | while | flops 1078329344 | bytes 14553285 | solution.py:90
  154.0 2.8 fusion.43
  156.8 1.8 fusion.44
  158.6 1.8 convolution_add_fusion.2
  160.4 3.4 fusion.45
  166.3 2.8 fusion.43
  169.1 1.7 fusion.44
  170.8 1.8 convolution_add_fusion.2
  172.6 3.3 fusion.45
  178.4 2.8 fusion.43
  181.2 1.7 fusion.44
  182.9 1.8 convolution_add_fusion.2
  184.7 3.3 fusion.45
  190.6 2.8 fusion.43
  193.3 1.7 fusion.44
  195.0 1.8 convolution_add_fusion.2
  196.8 3.3 fusion.45
  200.2 5.9 %pad_maximum_fusion = f32[64,260,128]{2,1,0:T(8,128)} fusion(f32[64,4,128]{2,1,0:T(4,128)S(1)} %broadcast_in_dim.39, f32[64,128,128]{2,1,0:T(8,128)} %bitcast.74, f32[64,128,128]{2,1,0:T(8,128)} %bitcast.16), kind=kLoop, calls=%fused_computation.18 | loop fusion | flops 4259840 | bytes 17039360 | tf_op jit(solution)/shard_map/concatenate | solution.py:92
  206.1 7.6 %all-to-all-start.1 = ((f32[64,260,128]{2,1,0:T(8,128)}), f32[64,260,128]{2,1,0:T(8,128)}, u32[]{:S(2)}, u32[]{:S(2)}) async-start(f32[64,260,128]{2,1,0:T(8,128)} %pad_maximum_fusion), calls=%async_computation.1 | async-start | bytes 17301504 | tf_op jit(solution)/shard_map/all_to_all | solution.py:101
  215.5 190.1 %all-to-all-done.1 = f32[64,260,128]{2,1,0:T(8,128)} async-done(((f32[64,260,128]{2,1,0:T(8,128)}), f32[64,260,128]{2,1,0:T(8,128)}, u32[]{:S(2)}, u32[]{:S(2)}) %all-to-all-start.1) | async-done | bytes 8519712 | tf_op jit(solution)/shard_map/all_to_all | solution.py:101
  405.6 3.9 reduce_sum.39
  410.1 21.2 %psum.7 = f32[512]{0:T(512)S(1)} all-reduce(f32[512]{0:T(512)S(1)} %slice_bitcast_fusion.2), channel_id=1, replica_groups=mesh['dp'=8,'seq'=64] {'dp'}, use_global_device_ids=true, to_apply=%region_7.8 | all-reduce | flops 512 | bytes 4096 | tf_op jit(solution)/shard_map/psum | solution.py:105
  (30 shorter events, 5.7 us)
Async XLA Ops:
  3.8 13.0 %copy-start.2 = (bf16[1,128,512]{2,1,0:T(8,128)(2,1)S(1)}, bf16[1,128,512]{2,1,0:T(8,128)(2,1)}, u32[]{:S(2)}) copy-start(bf16[1,128,512]{2,1,0:T(8,128)(2,1)} %param.7) | copy-start | bytes 393220
  3.8 13.1 %copy-start.1 = (bf16[1,128,512]{2,1,0:T(8,128)(2,1)S(1)}, bf16[1,128,512]{2,1,0:T(8,128)(2,1)}, u32[]{:S(2)}) copy-start(bf16[1,128,512]{2,1,0:T(8,128)(2,1)} %param.11) | copy-start | bytes 393220
  3.9 106.1 %all-to-all-start = ((bf16[64,128,256]{2,1,0:T(8,128)(2,1)}), bf16[64,128,256]{2,1,0:T(8,128)(2,1)}, u32[]{:S(2)}, u32[]{:S(2)}) async-start(bf16[64,128,256]{2,1,0:T(8,128)(2,1)} %broadcast_in_dim.36), calls=%async_computation | async-start | bytes 8388608 | tf_op jit(solution)/shard_map/all_to_all | solution.py:47
  132.7 13.7 %copy-start = (f32[8192,512]{1,0:T(8,128)S(1)}, f32[8192,512]{1,0:T(8,128)}, u32[]{:S(2)}) copy-start(f32[8192,512]{1,0:T(8,128)} %get-tuple-element.132) | copy-start | bytes 50331652
  132.7 13.7 %copy-start.3 = (f32[512]{0:T(512)S(1)}, f32[512]{0:T(512)}, u32[]{:S(2)}) copy-start(f32[512]{0:T(512)} %param.10) | copy-start | bytes 6148
  206.1 199.5 %all-to-all-start.1 = ((f32[64,260,128]{2,1,0:T(8,128)}), f32[64,260,128]{2,1,0:T(8,128)}, u32[]{:S(2)}, u32[]{:S(2)}) async-start(f32[64,260,128]{2,1,0:T(8,128)} %pad_maximum_fusion), calls=%async_computation.1 | async-start | bytes 17301504 | tf_op jit(solution)/shard_map/all_to_all | solution.py:101

commit v2 on v0

v2 whole, which is shorter than its diff:
```python
import math

import jax
import jax.numpy as jnp
from jax import lax
from jax.sharding import PartitionSpec as P

HEADS = 4
KEY = 128
VAL = 128


def to_rows(tokens, heads):
    positions = tokens.shape[0]
    width = tokens.shape[1] // heads
    return (
        tokens.reshape(positions, heads, width).transpose(1, 0, 2).reshape(heads * positions, width)
    )


def to_tokens(rows_in, heads):
    positions = rows_in.shape[0] // heads
    width = rows_in.shape[1]
    return (
        rows_in.reshape(heads, positions, width)
        .transpose(1, 0, 2)
        .reshape(positions, heads * width)
    )


def contract_first(left_mat, right_mat):
    return lax.dot_general(
        left_mat, right_mat, (((0,), (0,)), ((), ())), preferred_element_type=jnp.float32
    )


def contract_last(left_mat, right_mat):
    return lax.dot_general(
        left_mat, right_mat, (((1,), (1,)), ((), ())), preferred_element_type=jnp.float32
    )


def gather_seq(local, shards):
    return lax.all_to_all(
        jnp.broadcast_to(local[None], (shards,) + local.shape),
        "seq",
        split_axis=0,
        concat_axis=0,
        tiled=True,
    ).reshape(shards * local.shape[0], local.shape[1])


def reduce_seq(terms):
    return jnp.sum(lax.all_to_all(terms, "seq", split_axis=0, concat_axis=0, tiled=True), axis=0)


def body(query, key_in, value_in, out_gain, cotangent):
    positions = query.shape[1]
    shards = lax.axis_size("seq")
    groups = lax.axis_size("dp")
    key_mat = gather_seq(key_in[0], shards)
    value_mat = gather_seq(value_in[0], shards)
    score_scale = 1.0 / math.sqrt(KEY)
    query_rows = to_rows(query[0], HEADS)
    scores = contract_last(query_rows, key_mat) * score_scale
    row_top = jnp.max(scores, axis=1, keepdims=True)
    expo_rows = jnp.exp(scores - row_top)
    weights = (expo_rows / jnp.sum(expo_rows, axis=1, keepdims=True)).astype(jnp.bfloat16)
    out_rows = jnp.dot(weights, value_mat, preferred_element_type=jnp.float32)
    out_tokens = to_tokens(out_rows, HEADS)
    attended = (out_tokens * out_gain).astype(jnp.bfloat16)
    upstream = cotangent[0].astype(jnp.float32)
    gain_rows = jnp.sum(upstream * out_tokens, axis=0).reshape(HEADS, VAL)
    grad_out = (upstream * out_gain).astype(jnp.bfloat16)
    grad_rows = to_rows(grad_out, HEADS)
    delta_rows = jnp.sum(grad_rows.astype(jnp.float32) * out_rows, axis=1, keepdims=True)
    value_terms = contract_first(weights, grad_rows).reshape(shards, positions, VAL)
    value_recv = reduce_seq(
        jnp.concatenate(
            [value_terms, jnp.broadcast_to(gain_rows[None], (shards, HEADS, VAL))], axis=1
        )
    )
    grad_value = value_recv[:positions]
    gain_seq = value_recv[positions:]
    gain_total = jnp.sum(
        lax.all_to_all(
            jnp.broadcast_to(gain_seq[None], (groups,) + gain_seq.shape),
            "dp",
            split_axis=0,
            concat_axis=0,
            tiled=True,
        ),
        axis=0,
    ).reshape(HEADS * VAL)
    grad_gain = gain_total / math.sqrt(groups * shards * positions)
    d_prob = contract_last(grad_rows, value_mat)
    d_score = (weights.astype(jnp.float32) * (d_prob - delta_rows)).astype(jnp.bfloat16)
    query_acc = jnp.dot(d_score, key_mat, preferred_element_type=jnp.float32)
    key_terms = (contract_first(d_score, query_rows) * score_scale).reshape(shards, positions, KEY)
    grad_key = reduce_seq(key_terms)
    grad_query = to_tokens(query_acc * score_scale, HEADS).astype(jnp.bfloat16)
    return (
        attended[None],
        grad_query[None],
        grad_key.astype(jnp.bfloat16)[None],
        grad_value.astype(jnp.bfloat16)[None],
        grad_gain,
    )


def solution(mesh):
    placed = (
        P("dp", "seq", None),
        P("dp", "seq", None),
        P("dp", "seq", None),
        P(),
        P("dp", "seq", None),
    )
    return jax.shard_map(
        body,
        mesh=mesh,
        in_specs=placed,
        out_specs=(
            P("dp", "seq", None),
            P("dp", "seq", None),
            P("dp", "seq", None),
            P("dp", "seq", None),
            P(),
        ),
        check_vma=False,
    )
```

time: 1050 us -> 378 us (0.36)
  waiting for transfers between devices: 640 us -> 182 us
  blocking collectives: 271 us -> 61.6 us
  starting transfers between devices: 5.74 us -> 36.1 us
  matrix products: 61.4 us -> 39.2 us
  between operations: 14.1 us -> 0.8 us
  other arithmetic: 26.4 us -> 38.2 us
    all_gather x2 -> x0, waiting for transfers between devices: 638 us -> none  [the longest x1 326 us: body(): lax.all_gather(value_in, 'seq', axis=1, tiled=True)]
    psum x1 -> x0, blocking collectives: 211 us -> none  [body(): gain_total = lax.psum(jnp.sum(upstream * out_tokens, axis=0), ('dp', 'seq'))]
    all_to_all x1 -> x4, waiting for transfers between devices: 0.01 us -> 182 us  [the longest x2 151 us: reduce_seq(): lax.all_to_all(terms, 'seq', split_axis=0, concat_axis=0, tiled=True)]
    all_to_all x1 -> x4, starting transfers between devices: 5.66 us -> 36.1 us  [the longest x1 15.3 us: body(): lax.all_to_all(jnp.broadcast_to(gain_seq[None], (groups,) + gain_seq.shap...]
    dynamic_slice x12 -> x0, local copies, waits for them, and re-layouts: 24 us -> none  [the longest x8 21.7 us: score_grad(): weight_part = lax.dynamic_slice_in_dim(weights, offset_at, block_size, 1)]
    dot_general x0 -> x1, local copies, waits for them, and re-layouts: none -> 11.9 us  [contract_first(): lax.dot_general(left_mat, right_mat, (((0,), (0,)), ((), ())), preferred_...]
    dot_general x5 -> x2, matrix products: 25.2 us -> 14.2 us  [contract_last(): lax.dot_general(left_mat, right_mat, (((1,), (1,)), ((), ())), preferred_...]
  transfers between devices with their start and end apart: 3 -> 4, of which waited for: 2 -> 4; matrix products, arithmetic and copies ran while one was open for 3% -> 19% of each run, Pallas kernels for 0% -> 0%
where the time goes in v2:
time: 378 us; the launch traced here: 377 us
  waiting for transfers between devices  182 us (48%)
  blocking collectives  61.6 us (16%)
  matrix products  39.2 us (10%)
  other arithmetic  38.2 us (10%)
  starting transfers between devices  36.1 us (10%)
  local copies, waits for them, and re-layouts  18.6 us (5%)
    all_to_all x2, waiting for transfers between devices, reduce_seq(): lax.all_to_all(terms, 'seq', split_axis=0, concat_axis=0, tiled=True)  151 us
    all_to_all x1, blocking collectives, gather_seq(): lax.all_to_all(jnp.broadcast_to(local[None], (shards,) + local.shape), 's...  61.6 us
    all_to_all x1, waiting for transfers between devices, gather_seq(): lax.all_to_all(jnp.broadcast_to(local[None], (shards,) + local.shape), 's...  19.8 us
    all_to_all x1, starting transfers between devices, body(): lax.all_to_all(jnp.broadcast_to(gain_seq[None], (groups,) + gain_seq.shap...  15.3 us
    dot_general x2, matrix products, contract_last(): lax.dot_general(left_mat, right_mat, (((1,), (1,)), ((), ())), preferred_...  14.2 us
    all_to_all x2, starting transfers between devices, reduce_seq(): lax.all_to_all(terms, 'seq', split_axis=0, concat_axis=0, tiled=True)  14.2 us
    dot_general x2, matrix products, contract_first(): lax.dot_general(left_mat, right_mat, (((0,), (0,)), ((), ())), preferred_...  13.4 us
    dot_general x1, local copies, waits for them, and re-layouts, contract_first(): lax.dot_general(left_mat, right_mat, (((0,), (0,)), ((), ())), preferred_...  11.9 us
  transfers between devices with their start and end apart: 4, of which 4 were waited for; matrix products, arithmetic and copies ran while one was open for 19% of the time, Pallas kernels for 0%

profile of v2, /device:TPU:1, one launch (start us, length us, event | category | flops | bytes accessed | tf_op | source)
XLA Modules:
  0.0 376.7 jit_solution(15039736305173656012)
XLA Ops:
  0.7 1.3 broadcast_in_dim.15
  2.0 61.6 %all_to_all.25 = bf16[64,128,128]{2,1,0:T(8,128)(2,1)} all-to-all(bf16[64,128,128]{2,1,0:T(8,128)(2,1)S(1)} %broadcast_in_dim.15), channel_id=1, replica_groups=mesh['dp'=8,'seq'=64] {'seq'}, dimensions={0} | all-to-all | bytes 4194304 | tf_op jit(solution)/shard_map/all_to_all | solution.py:44
  63.5 2.7 broadcast_in_dim.17
  66.2 6.6 %all-to-all-start.1 = ((bf16[64,128,128]{2,1,0:T(8,128)(2,1)}), bf16[64,128,128]{2,1,0:T(8,128)(2,1)S(1)}, u32[]{:S(2)}, u32[]{:S(2)}) async-start(bf16[64,128,128]{2,1,0:T(8,128)(2,1)} %broadcast_in_dim.17), calls=%async_computation.1 | async-start | bytes 4194304 | tf_op jit(solution)/shard_map/all_to_all | solution.py:44
  73.1 0.1 copy.35
  73.2 9.6 %multiply_reduce_fusion = (f32[512]{0:T(512)S(1)}, f32[512,8192]{1,0:T(8,128)}) fusion(bf16[512,128]{1,0:T(8,128)(2,1)S(1)} %bitcast.54, bf16[8192,128]{1,0:T(8,128)(2,1)} %bitcast.49), kind=kOutput, calls=%fused_computation.3 | convolution fusion | flops 1082129920 | bytes 19007488 | tf_op jit(solution)/shard_map/dot_general | solution.py:38
  82.8 8.6 %fusion = f32[512]{0:T(512)S(1)} fusion(f32[512,8192]{1,0:T(8,128)} %get-tuple-element.8, f32[512]{0:T(512)S(1)} %get-tuple-element.7), kind=kLoop, calls=%fused_computation.4 | loop fusion | flops 12582400 | bytes 16781312 | tf_op jit(solution)/shard_map/reduce_sum | solution.py:68
  91.5 10.1 %divide_convert_fusion = bf16[512,8192]{1,0:T(8,128)(2,1)} fusion(f32[512,8192]{1,0:T(8,128)} %get-tuple-element.8, f32[512]{0:T(512)S(1)} %fusion, f32[512]{0:T(512)S(1)} %get-tuple-element.7), kind=kLoop, calls=%fused_computation.1 | loop fusion | flops 16777216 | bytes 25169920 | tf_op jit(solution)/shard_map/convert_element_type | solution.py:68
  101.6 19.8 %all-to-all-done.1 = bf16[64,128,128]{2,1,0:T(8,128)(2,1)S(1)} async-done(((bf16[64,128,128]{2,1,0:T(8,128)(2,1)}), bf16[64,128,128]{2,1,0:T(8,128)(2,1)S(1)}, u32[]{:S(2)}, u32[]{:S(2)}) %all-to-all-start.1) | async-done | bytes 2097184 | tf_op jit(solution)/shard_map/all_to_all | solution.py:44
  121.4 5.9 %multiply_reduce_fusion.1 = (f32[4,128]{1,0:T(4,128)S(1)}, bf16[128,4,128]{2,0,1:T(8,128)(2,1)S(1)}, f32[512,128]{1,0:T(8,128)S(1)}) fusion(f32[128,4,128]{2,1,0:T(4,128)S(1)} %reshape.116, f32[4,128]{1,0:T(4,128)S(1)} %bitcast.61, bf16[512,8192]{1,0:T(8,128)(2,1)} %divide_convert_fusion, bf16[8192,128]{1,0:T(8,128)(2,1)S(1)} %bitcast.47), kind=kOutput, calls=%fused_computation.9 | convolution fusion | flops 1074003456 | bytes 11145216 | tf_op jit(solution)/shard_map/dot_general | solution.py:69
  127.3 0.2 multiply_reduce_fusion.2
  127.5 4.5 %multiply_convert_fusion = bf16[512,8192]{1,0:T(8,128)(2,1)} fusion(bf16[512,8192]{1,0:T(8,128)(2,1)S(1)} %copy-done, bf16[512,128]{1,0:T(8,128)(2,1)S(1)} %bitcast.51, bf16[8192,128]{1,0:T(8,128)(2,1)S(1)} %bitcast.48, f32[512]{0:T(512)S(1)} %multiply_reduce_fusion.2), kind=kOutput, calls=%fused_computation | convolution fusion | flops 1090519040 | bytes 19007488 | tf_op jit(solution)/shard_map/dot_general | solution.py:38
  132.0 7.7 %convolution_multiply_fusion = f32[8192,128]{1,0:T(8,128)} fusion(bf16[512,8192]{1,0:T(8,128)(2,1)} %multiply_convert_fusion, bf16[512,128]{1,0:T(8,128)(2,1)S(1)} %bitcast.55), kind=kOutput, calls=%fused_computation.5 | convolution fusion | flops 1074790400 | bytes 12713984 | tf_op jit(solution)/shard_map/dot_general | solution.py:32
  139.7 6.7 %all-to-all-start.2 = ((f32[64,128,128]{2,1,0:T(8,128)}), f32[64,128,128]{2,1,0:T(8,128)}, u32[]{:S(2)}, u32[]{:S(2)}) async-start(f32[64,128,128]{2,1,0:T(8,128)} %bitcast.46), calls=%async_computation.2 | async-start | bytes 8388608 | tf_op jit(solution)/shard_map/all_to_all | solution.py:54
  146.4 10.1 %fusion.16 = bf16[8192,512]{0,1:T(8,128)(2,1)} fusion(f32[512]{0:T(512)S(1)} %fusion, f32[512]{0:T(512)S(1)} %get-tuple-element.7, f32[512,8192]{1,0:T(8,128)} %get-tuple-element.8), kind=kLoop, calls=%fused_computation.18 | loop fusion | flops 16777216 | bytes 25169920 | tf_op jit(solution)/shard_map/div | solution.py:68
  156.6 11.9 %copy.42 = bf16[8192,512]{1,0:T(8,128)(2,1)} copy(bf16[8192,512]{0,1:T(8,128)(2,1)} %fusion.16) | data formatting | bytes 16777216 | tf_op jit(solution)/shard_map/dot_general | solution.py:32
  168.5 5.7 %fusion.3 = f32[64,128,128]{2,1,0:T(8,128)S(1)} fusion(bf16[64,128,512]{2,1,0:T(8,128)(2,1)} %bitcast.45, bf16[512,128,1]{1,0,2:T(8,128)(2,1)S(1)} %bitcast.52), kind=kOutput, calls=%fused_computation.17 | convolution fusion | flops 1073741824 | bytes 12713984 | tf_op jit(solution)/shard_map/dot_general | solution.py:32
  174.3 2.4 pad_maximum_fusion
  176.7 63.1 %all-to-all-done.2 = f32[64,128,128]{2,1,0:T(8,128)} async-done(((f32[64,128,128]{2,1,0:T(8,128)}), f32[64,128,128]{2,1,0:T(8,128)}, u32[]{:S(2)}, u32[]{:S(2)}) %all-to-all-start.2) | async-done | bytes 4194336 | tf_op jit(solution)/shard_map/all_to_all | solution.py:54
  239.8 7.4 %all-to-all-start.3 = ((f32[64,132,128]{2,1,0:T(8,128)}), f32[64,132,128]{2,1,0:T(8,128)}, u32[]{:S(2)}, u32[]{:S(2)}) async-start(f32[64,132,128]{2,1,0:T(8,128)} %pad_maximum_fusion), calls=%async_computation.3 | async-start | bytes 8912896 | tf_op jit(solution)/shard_map/all_to_all | solution.py:54
  247.2 0.2 copy.36
  247.5 5.7 %fusion.1 = bf16[512,128]{1,0:T(8,128)(2,1)S(1)} fusion(bf16[512,8192]{1,0:T(8,128)(2,1)} %multiply_convert_fusion, bf16[8192,128]{1,0:T(8,128)(2,1)S(1)} %bitcast.50), kind=kOutput, calls=%fused_computation.8 | convolution fusion | flops 1073872896 | bytes 10616832 | tf_op jit(solution)/shard_map/dot_general | solution.py:98
  253.3 0.7 convert_element_type.79
  254.1 0.7 multiply_convert_fusion.2
  254.7 3.0 reduce_sum.56
  257.8 88.1 %all-to-all-done.3 = f32[64,132,128]{2,1,0:T(8,128)} async-done(((f32[64,132,128]{2,1,0:T(8,128)}), f32[64,132,128]{2,1,0:T(8,128)}, u32[]{:S(2)}, u32[]{:S(2)}) %all-to-all-start.3) | async-done | bytes 4325408 | tf_op jit(solution)/shard_map/all_to_all | solution.py:54
  345.8 2.5 reduce_sum.58
  348.3 0.6 broadcast_in_dim.20
  348.9 15.3 %all-to-all-start.4 = ((f32[8,4,128]{2,1,0:T(4,128)}), f32[8,4,128]{2,1,0:T(4,128)S(1)}, u32[]{:S(2)}, u32[]{:S(2)}) async-start(f32[8,4,128]{2,1,0:T(4,128)} %broadcast_in_dim.20), calls=%async_computation.4 | async-start | bytes 32768 | tf_op jit(solution)/shard_map/all_to_all | solution.py:86
  364.2 0.6 fusion.2
  364.9 11.3 %all-to-all-done.4 = f32[8,4,128]{2,1,0:T(4,128)S(1)} async-done(((f32[8,4,128]{2,1,0:T(4,128)}), f32[8,4,128]{2,1,0:T(4,128)S(1)}, u32[]{:S(2)}, u32[]{:S(2)}) %all-to-all-start.4) | async-done | bytes 16416 | tf_op jit(solution)/shard_map/all_to_all | solution.py:86
  376.1 0.6 multiply_bitcast_fusion
  (17 shorter events, 0.5 us)
Async XLA Ops:
  0.6 72.2 %copy-start.2 = (bf16[1,128,512]{2,1,0:T(8,128)(2,1)S(1)}, bf16[1,128,512]{2,1,0:T(8,128)(2,1)}, u32[]{:S(2)}) copy-start(bf16[1,128,512]{2,1,0:T(8,128)(2,1)} %param.9) | copy-start | bytes 393220
  0.6 72.3 %copy-start.3 = (bf16[1,128,512]{2,1,0:T(8,128)(2,1)S(1)}, bf16[1,128,512]{2,1,0:T(8,128)(2,1)}, u32[]{:S(2)}) copy-start(bf16[1,128,512]{2,1,0:T(8,128)(2,1)} %param.5) | copy-start | bytes 393220
  66.2 55.3 %all-to-all-start.1 = ((bf16[64,128,128]{2,1,0:T(8,128)(2,1)}), bf16[64,128,128]{2,1,0:T(8,128)(2,1)S(1)}, u32[]{:S(2)}, u32[]{:S(2)}) async-start(bf16[64,128,128]{2,1,0:T(8,128)(2,1)} %broadcast_in_dim.17), calls=%async_computation.1 | async-start | bytes 4194304 | tf_op jit(solution)/shard_map/all_to_all | solution.py:44
  91.5 30.0 %copy-start.4 = (f32[512]{0:T(512)S(1)}, f32[512]{0:T(512)}, u32[]{:S(2)}) copy-start(f32[512]{0:T(512)} %param.8) | copy-start | bytes 6148
  121.4 6.0 %copy-start = (bf16[512,8192]{1,0:T(8,128)(2,1)S(1)}, bf16[512,8192]{1,0:T(8,128)(2,1)}, u32[]{:S(2)}) copy-start(bf16[512,8192]{1,0:T(8,128)(2,1)} %divide_convert_fusion) | copy-start | bytes 25165828
  139.7 100.0 %all-to-all-start.2 = ((f32[64,128,128]{2,1,0:T(8,128)}), f32[64,128,128]{2,1,0:T(8,128)}, u32[]{:S(2)}, u32[]{:S(2)}) async-start(f32[64,128,128]{2,1,0:T(8,128)} %bitcast.46), calls=%async_computation.2 | async-start | bytes 8388608 | tf_op jit(solution)/shard_map/all_to_all | solution.py:54
  174.3 73.2 %copy-start.1 = (bf16[64,128,128]{2,1,0:T(8,128)(2,1)S(1)}, bf16[64,128,128]{2,1,0:T(8,128)(2,1)}, u32[]{:S(2)}) copy-start(bf16[64,128,128]{2,1,0:T(8,128)(2,1)} %all_to_all.25) | copy-start | bytes 6291460
  239.8 106.1 %all-to-all-start.3 = ((f32[64,132,128]{2,1,0:T(8,128)}), f32[64,132,128]{2,1,0:T(8,128)}, u32[]{:S(2)}, u32[]{:S(2)}) async-start(f32[64,132,128]{2,1,0:T(8,128)} %pad_maximum_fusion), calls=%async_computation.3 | async-start | bytes 8912896 | tf_op jit(solution)/shard_map/all_to_all | solution.py:54
  348.9 27.2 %all-to-all-start.4 = ((f32[8,4,128]{2,1,0:T(4,128)}), f32[8,4,128]{2,1,0:T(4,128)S(1)}, u32[]{:S(2)}, u32[]{:S(2)}) async-start(f32[8,4,128]{2,1,0:T(4,128)} %broadcast_in_dim.20), calls=%async_computation.4 | async-start | bytes 32768 | tf_op jit(solution)/shard_map/all_to_all | solution.py:86

commit v3 on v2

--- a/solution.py
+++ b/solution.py
@@ -3,7 +3,7 @@
 import jax
 import jax.numpy as jnp
 from jax import lax
-from jax.sharding import PartitionSpec as P
+from jax.sharding import Mesh, PartitionSpec as P
 
 HEADS = 4
 KEY = 128
@@ -43,7 +43,7 @@
 def gather_seq(local, shards):
     return lax.all_to_all(
         jnp.broadcast_to(local[None], (shards,) + local.shape),
-        "seq",
+        SEQ_AXES,
         split_axis=0,
         concat_axis=0,
         tiled=True,
@@ -51,12 +51,24 @@
 
 
 def reduce_seq(terms):
-    return jnp.sum(lax.all_to_all(terms, "seq", split_axis=0, concat_axis=0, tiled=True), axis=0)
+    return jnp.sum(lax.all_to_all(terms, SEQ_AXES, split_axis=0, concat_axis=0, tiled=True), axis=0)
+
+
+SEQ_AXES = ("sz", "sy", "sx")
+
+
+def scatter_seq(terms, sides):
+    grid = terms.reshape(sides + (-1,) + terms.shape[1:])
+    for depth in range(len(sides) - 1, -1, -1):
+        grid = jnp.moveaxis(grid, depth, 0)
+        grid = lax.psum_scatter(grid, SEQ_AXES[depth], scatter_dimension=0, tiled=True)[0]
+    return grid
 
 
 def body(query, key_in, value_in, out_gain, cotangent):
     positions = query.shape[1]
-    shards = lax.axis_size("seq")
+    shards = lax.axis_size(SEQ_AXES)
+    sides = tuple(lax.axis_size(name) for name in SEQ_AXES)
     groups = lax.axis_size("dp")
     key_mat = gather_seq(key_in[0], shards)
     value_mat = gather_seq(value_in[0], shards)
@@ -74,30 +86,27 @@
     grad_out = (upstream * out_gain).astype(jnp.bfloat16)
     grad_rows = to_rows(grad_out, HEADS)
     delta_rows = jnp.sum(grad_rows.astype(jnp.float32) * out_rows, axis=1, keepdims=True)
-    value_terms = contract_first(weights, grad_rows).reshape(shards, positions, VAL)
-    value_recv = reduce_seq(
-        jnp.concatenate(
-            [value_terms, jnp.broadcast_to(gain_rows[None], (shards, HEADS, VAL))], axis=1
-        )
-    )
-    grad_value = value_recv[:positions]
-    gain_seq = value_recv[positions:]
-    gain_total = jnp.sum(
+    gain_dp = jnp.sum(
         lax.all_to_all(
-            jnp.broadcast_to(gain_seq[None], (groups,) + gain_seq.shape),
+            jnp.broadcast_to(gain_rows[None], (groups,) + gain_rows.shape),
             "dp",
             split_axis=0,
             concat_axis=0,
             tiled=True,
         ),
         axis=0,
-    ).reshape(HEADS * VAL)
-    grad_gain = gain_total / math.sqrt(groups * shards * positions)
+    )
+    value_terms = contract_first(weights, grad_rows)
+    grad_value = scatter_seq(value_terms, sides)
     d_prob = contract_last(grad_rows, value_mat)
     d_score = (weights.astype(jnp.float32) * (d_prob - delta_rows)).astype(jnp.bfloat16)
     query_acc = jnp.dot(d_score, key_mat, preferred_element_type=jnp.float32)
     key_terms = (contract_first(d_score, query_rows) * score_scale).reshape(shards, positions, KEY)
-    grad_key = reduce_seq(key_terms)
+    key_recv = reduce_seq(
+        jnp.concatenate([key_terms, jnp.broadcast_to(gain_dp[None], (shards, HEADS, KEY))], axis=1)
+    )
+    grad_key = key_recv[:positions]
+    grad_gain = key_recv[positions:].reshape(HEADS * VAL) / math.sqrt(groups * shards * positions)
     grad_query = to_tokens(query_acc * score_scale, HEADS).astype(jnp.bfloat16)
     return (
         attended[None],
@@ -109,23 +118,16 @@
 
 
 def solution(mesh):
-    placed = (
-        P("dp", "seq", None),
-        P("dp", "seq", None),
-        P("dp", "seq", None),
-        P(),
-        P("dp", "seq", None),
+    sides = (4, 4, 4) if mesh.shape["seq"] == 64 else None
+    split_mesh = Mesh(
+        mesh.devices.reshape((mesh.shape["dp"],) + sides), ("dp",) + SEQ_AXES
     )
+    tokens = P("dp", SEQ_AXES, None)
+    placed = (tokens, tokens, tokens, P(), tokens)
     return jax.shard_map(
         body,
-        mesh=mesh,
+        mesh=split_mesh,
         in_specs=placed,
-        out_specs=(
-            P("dp", "seq", None),
-            P("dp", "seq", None),
-            P("dp", "seq", None),
-            P("dp", "seq", None),
-            P(),
-        ),
+        out_specs=(tokens, tokens, tokens, tokens, P()),
         check_vma=False,
     )

time: 378 us -> 441 us (1.17)
  waiting for transfers between devices: 182 us -> 229 us
  between operations: 0.8 us -> 13.9 us
  local copies, waits for them, and re-layouts: 18.6 us -> 29.7 us
  starting transfers between devices: 36.1 us -> 27.4 us
    unnamed x0 -> x5, waiting for transfers between devices: none -> 185 us
    all_to_all x4 -> x3, waiting for transfers between devices: 182 us -> 20 us  [the longest x1 20 us: gather_seq(): lax.all_to_all(jnp.broadcast_to(local[None], (shards,) + local.shape), SE...]
    reduce_scatter x0 -> x1, waiting for transfers between devices: none -> 23.8 us  [scatter_seq(): lax.psum_scatter(grid, SEQ_AXES[depth], scatter_dimension=0, tiled=True)[0]]
    all_to_all x4 -> x3, starting transfers between devices: 36.1 us -> 27.3 us  [the longest x1 15.2 us: body(): lax.all_to_all(jnp.broadcast_to(gain_rows[None], (groups,) + gain_rows.sh...]
    unnamed x11 -> x13, local copies, waits for them, and re-layouts: 0.14 us -> 5.88 us
  transfers between devices with their start and end apart: 4 -> 6, of which waited for: 4 -> 4; matrix products, arithmetic and copies ran while one was open for 19% -> 19% of each run, Pallas kernels for 0% -> 0%
where the time goes in v3:
time: 441 us; the launch traced here: 438 us
  waiting for transfers between devices  229 us (52%)
  blocking collectives  61.6 us (14%)
  other arithmetic  38.9 us (9%)
  matrix products  38 us (9%)
  local copies, waits for them, and re-layouts  29.7 us (7%)
  starting transfers between devices  27.4 us (6%)
  between operations  13.9 us (3%)
    unnamed x5, waiting for transfers between devices  185 us
    all_to_all x1, blocking collectives, gather_seq(): lax.all_to_all(jnp.broadcast_to(local[None], (shards,) + local.shape), SE...  61.6 us
    reduce_scatter x1, waiting for transfers between devices, scatter_seq(): lax.psum_scatter(grid, SEQ_AXES[depth], scatter_dimension=0, tiled=True)[0]  23.8 us
    all_to_all x1, waiting for transfers between devices, gather_seq(): lax.all_to_all(jnp.broadcast_to(local[None], (shards,) + local.shape), SE...  20 us
    all_to_all x1, starting transfers between devices, body(): lax.all_to_all(jnp.broadcast_to(gain_rows[None], (groups,) + gain_rows.sh...  15.2 us
    dot_general x2, matrix products, contract_last(): lax.dot_general(left_mat, right_mat, (((1,), (1,)), ((), ())), preferred_...  14.4 us
    dot_general x2, matrix products, contract_first(): lax.dot_general(left_mat, right_mat, (((0,), (0,)), ((), ())), preferred_...  12.2 us
    dot_general x1, local copies, waits for them, and re-layouts, contract_first(): lax.dot_general(left_mat, right_mat, (((0,), (0,)), ((), ())), preferred_...  11.9 us
  transfers between devices with their start and end apart: 6, of which 4 were waited for; matrix products, arithmetic and copies ran while one was open for 19% of the time, Pallas kernels for 0%

profile of v3, /device:TPU:1, one launch (start us, length us, event | category | flops | bytes accessed | tf_op | source)
XLA Modules:
  0.0 438.1 jit_solution(9470266927720687964)
XLA Ops:
  7.2 1.3 broadcast_in_dim.15
  8.5 61.6 %all_to_all.20 = bf16[64,128,128]{2,1,0:T(8,128)(2,1)} all-to-all(bf16[64,128,128]{2,1,0:T(8,128)(2,1)S(1)} %broadcast_in_dim.15), channel_id=1, replica_groups=mesh['dp'=8,'sz'=4,'sy'=4,'sx'=4] {'sz','sy','sx'}, dimensions={0} | all-to-all | bytes 4194304 | tf_op jit(solution)/shard_map/all_to_all | solution.py:44
  70.0 2.7 broadcast_in_dim.17
  72.7 6.5 %all-to-all-start.1 = ((bf16[64,128,128]{2,1,0:T(8,128)(2,1)}), bf16[64,128,128]{2,1,0:T(8,128)(2,1)S(1)}, u32[]{:S(2)}, u32[]{:S(2)}) async-start(bf16[64,128,128]{2,1,0:T(8,128)(2,1)} %broadcast_in_dim.17), calls=%async_computation.1 | async-start | bytes 4194304 | tf_op jit(solution)/shard_map/all_to_all | solution.py:44
  79.5 9.6 %multiply_reduce_fusion = (f32[512]{0:T(512)S(1)}, f32[512,8192]{1,0:T(8,128)}) fusion(bf16[512,128]{1,0:T(8,128)(2,1)S(1)} %bitcast.75, bf16[8192,128]{1,0:T(8,128)(2,1)} %bitcast.70), kind=kOutput, calls=%fused_computation.3 | convolution fusion | flops 1082129920 | bytes 19007488 | tf_op jit(solution)/shard_map/dot_general | solution.py:38
  89.2 8.6 %fusion = f32[512]{0:T(512)S(1)} fusion(f32[512,8192]{1,0:T(8,128)} %get-tuple-element.8, f32[512]{0:T(512)S(1)} %get-tuple-element.7), kind=kLoop, calls=%fused_computation.4 | loop fusion | flops 12582400 | bytes 16781312 | tf_op jit(solution)/shard_map/reduce_sum | solution.py:80
  97.8 10.1 %divide_convert_fusion = bf16[512,8192]{1,0:T(8,128)(2,1)} fusion(f32[512,8192]{1,0:T(8,128)} %get-tuple-element.8, f32[512]{0:T(512)S(1)} %fusion, f32[512]{0:T(512)S(1)} %get-tuple-element.7), kind=kLoop, calls=%fused_computation.1 | loop fusion | flops 16777216 | bytes 25169920 | tf_op jit(solution)/shard_map/convert_element_type | solution.py:80
  108.0 20.0 %all-to-all-done.1 = bf16[64,128,128]{2,1,0:T(8,128)(2,1)S(1)} async-done(((bf16[64,128,128]{2,1,0:T(8,128)(2,1)}), bf16[64,128,128]{2,1,0:T(8,128)(2,1)S(1)}, u32[]{:S(2)}, u32[]{:S(2)}) %all-to-all-start.1) | async-done | bytes 2097184 | tf_op jit(solution)/shard_map/all_to_all | solution.py:44
  128.0 5.7 %multiply_reduce_fusion.1 = (f32[4,128]{1,0:T(4,128)S(1)}, bf16[128,4,128]{2,0,1:T(8,128)(2,1)S(1)}, f32[512,128]{1,0:T(8,128)S(1)}) fusion(f32[128,4,128]{2,1,0:T(4,128)S(1)} %reshape.108, f32[4,128]{1,0:T(4,128)S(1)} %bitcast.81, bf16[512,8192]{1,0:T(8,128)(2,1)} %divide_convert_fusion, bf16[8192,128]{1,0:T(8,128)(2,1)S(1)} %bitcast.68), kind=kOutput, calls=%fused_computation.12 | convolution fusion | flops 1074003456 | bytes 11145216 | tf_op jit(solution)/shard_map/dot_general | solution.py:81
  133.7 0.6 broadcast_in_dim.18
  134.3 15.2 %all-to-all-start.2 = ((f32[8,4,128]{2,1,0:T(4,128)}), f32[8,4,128]{2,1,0:T(4,128)S(1)}, u32[]{:S(2)}, u32[]{:S(2)}) async-start(f32[8,4,128]{2,1,0:T(4,128)} %broadcast_in_dim.18), calls=%async_computation.2 | async-start | bytes 32768 | tf_op jit(solution)/shard_map/all_to_all | solution.py:90
  149.6 4.8 %multiply_convert_fusion = bf16[512,8192]{1,0:T(8,128)(2,1)S(1)} fusion(bf16[512,8192]{1,0:T(8,128)(2,1)} %divide_convert_fusion, bf16[512,128]{1,0:T(8,128)(2,1)S(1)} %bitcast.72, bf16[8192,128]{1,0:T(8,128)(2,1)S(1)} %bitcast.69, f32[512]{0:T(512)S(1)} %multiply_reduce_fusion.2), kind=kOutput, calls=%fused_computation | convolution fusion | flops 1090519040 | bytes 19007488 | tf_op jit(solution)/shard_map/dot_general | solution.py:38
  154.4 3.2 copy-done
  157.6 4.4 convolution_multiply_fusion
  162.0 4.7 %pad_maximum_fusion = f32[64,132,128]{2,1,0:T(8,128)} fusion(f32[64,4,128]{2,1,0:T(4,128)S(1)} %broadcast_in_dim.19, f32[64,128,128]{2,1,0:T(8,128)} %bitcast.67), kind=kLoop, calls=%fused_computation.6 | loop fusion | flops 1081344 | bytes 8650752 | tf_op jit(solution)/shard_map/concatenate | solution.py:106
  166.7 5.7 %all-to-all-start.3 = ((f32[64,132,128]{2,1,0:T(8,128)}), f32[64,132,128]{2,1,0:T(8,128)}, u32[]{:S(2)}, u32[]{:S(2)}) async-start(f32[64,132,128]{2,1,0:T(8,128)} %pad_maximum_fusion), calls=%async_computation.3 | async-start | bytes 8912896 | tf_op jit(solution)/shard_map/all_to_all | solution.py:54
  172.5 10.1 %fusion.16 = bf16[8192,512]{0,1:T(8,128)(2,1)} fusion(f32[512]{0:T(512)S(1)} %fusion, f32[512]{0:T(512)S(1)} %get-tuple-element.7, f32[512,8192]{1,0:T(8,128)} %get-tuple-element.8), kind=kLoop, calls=%fused_computation.20 | loop fusion | flops 16777216 | bytes 25169920 | tf_op jit(solution)/shard_map/div | solution.py:80
  182.6 11.9 %copy.50 = bf16[8192,512]{1,0:T(8,128)(2,1)} copy(bf16[8192,512]{0,1:T(8,128)(2,1)} %fusion.16) | data formatting | bytes 16777216 | tf_op jit(solution)/shard_map/dot_general | solution.py:32
  194.5 7.8 %convolution_bitcast_fusion = f32[4,4,4,128,128]{4,3,0,2,1:T(8,128)} fusion(bf16[4,4,4,128,512]{4,3,2,1,0:T(8,128)(2,1)} %bitcast.66, bf16[512,128,1,1,1]{1,0,4,3,2:T(8,128)(2,1)S(1)} %bitcast.73), kind=kOutput, calls=%fused_computation.7 | convolution fusion | flops 1073741824 | bytes 12713984 | tf_op jit(solution)/shard_map/dot_general | solution.py:32
  202.4 1.3 dynamic-slice
  203.7 126.0 %all-reduce.5.cloned.1.call-done = f32[4,4,4,128,128]{4,3,0,2,1:T(8,128)} async-done(((f32[4,4,4,128,128]{4,3,0,2,1:T(8,128)}), f32[4,4,4,128,128]{4,3,0,2,1:T(8,128)}) %all-reduce.5.cloned.1.call-update) | async-done | bytes 4194320
  329.7 3.0 dynamic-slice_bitcast_fusion
  332.8 1.3 dynamic-slice.2
  334.0 58.7 %all-reduce.7.cloned.1.call-done = f32[4,4,128,128]{3,2,0,1:T(8,128)} async-done(((f32[4,4,128,128]{3,2,0,1:T(8,128)}), f32[4,4,128,128]{3,2,0,1:T(8,128)}) %all-reduce.7.cloned.1.call-update) | async-done | bytes 1048592
  392.7 2.3 dynamic-slice_bitcast_fusion.1
  395.1 5.7 %fusion.1 = bf16[512,128]{1,0:T(8,128)(2,1)S(1)} fusion(bf16[512,8192]{1,0:T(8,128)(2,1)} %copy-done, bf16[8192,128]{1,0:T(8,128)(2,1)S(1)} %bitcast.71), kind=kOutput, calls=%fused_computation.9 | convolution fusion | flops 1073872896 | bytes 10616832 | tf_op jit(solution)/shard_map/dot_general | solution.py:103
  401.2 0.7 convert_element_type.70
  401.9 0.7 multiply_convert_fusion.2
  402.6 23.8 %reduce-scatter.8.cloned.1.call-done = f32[1,128,128]{2,1,0:T(8,128)} async-done(((f32[4,128,128]{2,1,0:T(8,128)}), f32[1,128,128]{2,1,0:T(8,128)}) %reduce-scatter.8.cloned.1.call-update) | async-done | bytes 65552 | tf_op jit(solution)/shard_map/reduce_scatter | solution.py:64
  426.4 1.5 convert_element_type.71
  427.9 2.5 reduce_sum.49
  430.4 0.6 fusion.2
  (27 shorter events, 1.7 us)
Async XLA Ops:
  7.2 72.0 %copy-start.2 = (bf16[1,128,512]{2,1,0:T(8,128)(2,1)S(1)}, bf16[1,128,512]{2,1,0:T(8,128)(2,1)}, u32[]{:S(2)}) copy-start(bf16[1,128,512]{2,1,0:T(8,128)(2,1)} %param.9) | copy-start | bytes 393220
  7.2 72.1 %copy-start.3 = (bf16[1,128,512]{2,1,0:T(8,128)(2,1)S(1)}, bf16[1,128,512]{2,1,0:T(8,128)(2,1)}, u32[]{:S(2)}) copy-start(bf16[1,128,512]{2,1,0:T(8,128)(2,1)} %param.5) | copy-start | bytes 393220
  72.7 55.3 %all-to-all-start.1 = ((bf16[64,128,128]{2,1,0:T(8,128)(2,1)}), bf16[64,128,128]{2,1,0:T(8,128)(2,1)S(1)}, u32[]{:S(2)}, u32[]{:S(2)}) async-start(bf16[64,128,128]{2,1,0:T(8,128)(2,1)} %broadcast_in_dim.17), calls=%async_computation.1 | async-start | bytes 4194304 | tf_op jit(solution)/shard_map/all_to_all | solution.py:44
  97.8 30.2 %copy-start.4 = (f32[512]{0:T(512)S(1)}, f32[512]{0:T(512)}, u32[]{:S(2)}) copy-start(f32[512]{0:T(512)} %param.8) | copy-start | bytes 6148
  134.3 27.7 %all-to-all-start.2 = ((f32[8,4,128]{2,1,0:T(4,128)}), f32[8,4,128]{2,1,0:T(4,128)S(1)}, u32[]{:S(2)}, u32[]{:S(2)}) async-start(f32[8,4,128]{2,1,0:T(4,128)} %broadcast_in_dim.18), calls=%async_computation.2 | async-start | bytes 32768 | tf_op jit(solution)/shard_map/all_to_all | solution.py:90
  154.4 3.2 copy-start
  166.7 261.1 %all-to-all-start.3 = ((f32[64,132,128]{2,1,0:T(8,128)}), f32[64,132,128]{2,1,0:T(8,128)}, u32[]{:S(2)}, u32[]{:S(2)}) async-start(f32[64,132,128]{2,1,0:T(8,128)} %pad_maximum_fusion), calls=%async_computation.3 | async-start | bytes 8912896 | tf_op jit(solution)/shard_map/all_to_all | solution.py:54
  172.4 157.3 %all-reduce.5.cloned.1.call-start = ((), (), s32[]{:S(2)}) async-start(), calls=%async_computation.6 | async-start | bytes 8388608
  194.5 200.5 %copy-start.1 = (bf16[64,128,128]{2,1,0:T(8,128)(2,1)S(1)}, bf16[64,128,128]{2,1,0:T(8,128)(2,1)}, u32[]{:S(2)}) copy-start(bf16[64,128,128]{2,1,0:T(8,128)(2,1)} %all_to_all.20) | copy-start | bytes 6291460
  202.4 190.3 %all-reduce.7.cloned.1.call-start = ((), (), s32[]{:S(2)}) async-start(), calls=%async_computation.7 | async-start | bytes 2097152
  332.7 93.7 %reduce-scatter.8.cloned.1.call-start = ((), (), s32[]{:S(2)}) async-start(), calls=%async_computation.5 | async-start | bytes 327680 | tf_op jit(solution)/shard_map/reduce_scatter | solution.py:64
Sparse Core Ops, SparseCore 0:
  202.5 127.1 all-reduce.4
  332.8 59.8 all-reduce.6
  395.5 30.8 reduce-scatter.7

commit v4 on v2

--- a/solution.py
+++ b/solution.py
@@ -75,13 +75,16 @@
     grad_rows = to_rows(grad_out, HEADS)
     delta_rows = jnp.sum(grad_rows.astype(jnp.float32) * out_rows, axis=1, keepdims=True)
     value_terms = contract_first(weights, grad_rows).reshape(shards, positions, VAL)
-    value_recv = reduce_seq(
-        jnp.concatenate(
-            [value_terms, jnp.broadcast_to(gain_rows[None], (shards, HEADS, VAL))], axis=1
-        )
+    grad_value = reduce_seq(value_terms)
+    d_prob = contract_last(grad_rows, value_mat)
+    d_score = (weights.astype(jnp.float32) * (d_prob - delta_rows)).astype(jnp.bfloat16)
+    query_acc = jnp.dot(d_score, key_mat, preferred_element_type=jnp.float32)
+    key_terms = (contract_first(d_score, query_rows) * score_scale).reshape(shards, positions, KEY)
+    key_recv = reduce_seq(
+        jnp.concatenate([key_terms, jnp.broadcast_to(gain_rows[None], (shards, HEADS, KEY))], axis=1)
     )
-    grad_value = value_recv[:positions]
-    gain_seq = value_recv[positions:]
+    grad_key = key_recv[:positions]
+    gain_seq = key_recv[positions:]
     gain_total = jnp.sum(
         lax.all_to_all(
             jnp.broadcast_to(gain_seq[None], (groups,) + gain_seq.shape),
@@ -93,11 +96,6 @@
         axis=0,
     ).reshape(HEADS * VAL)
     grad_gain = gain_total / math.sqrt(groups * shards * positions)
-    d_prob = contract_last(grad_rows, value_mat)
-    d_score = (weights.astype(jnp.float32) * (d_prob - delta_rows)).astype(jnp.bfloat16)
-    query_acc = jnp.dot(d_score, key_mat, preferred_element_type=jnp.float32)
-    key_terms = (contract_first(d_score, query_rows) * score_scale).reshape(shards, positions, KEY)
-    grad_key = reduce_seq(key_terms)
     grad_query = to_tokens(query_acc * score_scale, HEADS).astype(jnp.bfloat16)
     return (
         attended[None],

time: 378 us -> 375 us (level)
  matrix products: 39.2 us -> 32.7 us
  starting transfers between devices: 36.1 us -> 40 us
    all_to_all x1, waiting for transfers between devices: 19.8 us -> 0.01 us  [gather_seq(): lax.all_to_all(jnp.broadcast_to(local[None], (shards,) + local.shape), 's...]
    all_to_all x2, waiting for transfers between devices: 151 us -> 171 us  [reduce_seq(): lax.all_to_all(terms, 'seq', split_axis=0, concat_axis=0, tiled=True)]
    dot_general x2, matrix products: 13.4 us -> 6.68 us  [contract_first(): lax.dot_general(left_mat, right_mat, (((0,), (0,)), ((), ())), preferred_...]
    all_to_all x2, starting transfers between devices: 14.2 us -> 18 us  [reduce_seq(): lax.all_to_all(terms, 'seq', split_axis=0, concat_axis=0, tiled=True)]
  transfers between devices with their start and end apart: 4 -> 4, of which waited for: 4 -> 3; matrix products, arithmetic and copies ran while one was open for 19% -> 19% of each run, Pallas kernels for 0% -> 0%
where the time goes in v4:
time: 375 us; the launch traced here: 374 us
  waiting for transfers between devices  182 us (49%)
  blocking collectives  61.6 us (16%)
  starting transfers between devices  40 us (11%)
  other arithmetic  38.2 us (10%)
  matrix products  32.7 us (9%)
  local copies, waits for them, and re-layouts  19.3 us (5%)
    all_to_all x2, waiting for transfers between devices, reduce_seq(): lax.all_to_all(terms, 'seq', split_axis=0, concat_axis=0, tiled=True)  171 us
    all_to_all x1, blocking collectives, gather_seq(): lax.all_to_all(jnp.broadcast_to(local[None], (shards,) + local.shape), 's...  61.6 us
    all_to_all x2, starting transfers between devices, reduce_seq(): lax.all_to_all(terms, 'seq', split_axis=0, concat_axis=0, tiled=True)  18 us
    all_to_all x1, starting transfers between devices, body(): lax.all_to_all(jnp.broadcast_to(gain_seq[None], (groups,) + gain_seq.shap...  15.3 us
    dot_general x2, matrix products, contract_last(): lax.dot_general(left_mat, right_mat, (((1,), (1,)), ((), ())), preferred_...  14.4 us
    dot_general x1, local copies, waits for them, and re-layouts, contract_first(): lax.dot_general(left_mat, right_mat, (((0,), (0,)), ((), ())), preferred_...  11.9 us
    all_to_all x1, waiting for transfers between devices, body(): lax.all_to_all(jnp.broadcast_to(gain_seq[None], (groups,) + gain_seq.shap...  11.3 us
    convert_element_type x1, other arithmetic, body(): (expo_rows / jnp.sum(expo_rows, axis=1, keepdims=True)).astype(jnp.bfloat16)  10.1 us
  transfers between devices with their start and end apart: 4, of which 3 were waited for; matrix products, arithmetic and copies ran while one was open for 19% of the time, Pallas kernels for 0%

profile of v4, /device:TPU:1, one launch (start us, length us, event | category | flops | bytes accessed | tf_op | source)
XLA Modules:
  0.0 374.4 jit_solution(15376889948616015745)
XLA Ops:
  0.7 1.3 broadcast_in_dim.15
  2.0 61.6 %all_to_all.25 = bf16[64,128,128]{2,1,0:T(8,128)(2,1)} all-to-all(bf16[64,128,128]{2,1,0:T(8,128)(2,1)S(1)} %broadcast_in_dim.15), channel_id=1, replica_groups=mesh['dp'=8,'seq'=64] {'seq'}, dimensions={0} | all-to-all | bytes 4194304 | tf_op jit(solution)/shard_map/all_to_all | solution.py:44
  63.5 2.6 broadcast_in_dim.17
  66.1 6.6 %all-to-all-start.1 = ((bf16[64,128,128]{2,1,0:T(8,128)(2,1)}), bf16[64,128,128]{2,1,0:T(8,128)(2,1)S(1)}, u32[]{:S(2)}, u32[]{:S(2)}) async-start(bf16[64,128,128]{2,1,0:T(8,128)(2,1)} %broadcast_in_dim.17), calls=%async_computation.1 | async-start | bytes 4194304 | tf_op jit(solution)/shard_map/all_to_all | solution.py:44
  73.0 0.1 copy.35
  73.2 9.6 %multiply_reduce_fusion = (f32[512]{0:T(512)S(1)}, f32[512,8192]{1,0:T(8,128)}) fusion(bf16[512,128]{1,0:T(8,128)(2,1)S(1)} %bitcast.54, bf16[8192,128]{1,0:T(8,128)(2,1)} %bitcast.49), kind=kOutput, calls=%fused_computation.3 | convolution fusion | flops 1082129920 | bytes 19007488 | tf_op jit(solution)/shard_map/dot_general | solution.py:38
  82.8 8.6 %fusion = f32[512]{0:T(512)S(1)} fusion(f32[512,8192]{1,0:T(8,128)} %get-tuple-element.8, f32[512]{0:T(512)S(1)} %get-tuple-element.7), kind=kLoop, calls=%fused_computation.4 | loop fusion | flops 12582400 | bytes 16781312 | tf_op jit(solution)/shard_map/reduce_sum | solution.py:68
  91.4 10.1 %fusion.16 = bf16[8192,512]{0,1:T(8,128)(2,1)} fusion(f32[512]{0:T(512)S(1)} %fusion, f32[512]{0:T(512)S(1)} %get-tuple-element.7, f32[512,8192]{1,0:T(8,128)} %get-tuple-element.8), kind=kLoop, calls=%fused_computation.18 | loop fusion | flops 16777216 | bytes 25169920 | tf_op jit(solution)/shard_map/div | solution.py:68
  101.6 11.9 %copy.42 = bf16[8192,512]{1,0:T(8,128)(2,1)} copy(bf16[8192,512]{0,1:T(8,128)(2,1)} %fusion.16) | data formatting | bytes 16777216 | tf_op jit(solution)/shard_map/dot_general | solution.py:32
  113.5 10.1 %divide_convert_fusion = bf16[512,8192]{1,0:T(8,128)(2,1)} fusion(f32[512,8192]{1,0:T(8,128)} %get-tuple-element.8, f32[512]{0:T(512)S(1)} %fusion, f32[512]{0:T(512)S(1)} %get-tuple-element.7), kind=kLoop, calls=%fused_computation.1 | loop fusion | flops 16777216 | bytes 25169920 | tf_op jit(solution)/shard_map/convert_element_type | solution.py:68
  123.6 5.9 %multiply_reduce_fusion.1 = (f32[4,128]{1,0:T(4,128)S(1)}, bf16[128,4,128]{2,0,1:T(8,128)(2,1)S(1)}, f32[512,128]{1,0:T(8,128)S(1)}) fusion(f32[128,4,128]{2,1,0:T(4,128)S(1)} %reshape.116, f32[4,128]{1,0:T(4,128)S(1)} %bitcast.61, bf16[512,8192]{1,0:T(8,128)(2,1)} %divide_convert_fusion, bf16[8192,128]{1,0:T(8,128)(2,1)S(1)} %bitcast.47), kind=kOutput, calls=%fused_computation.9 | convolution fusion | flops 1074003456 | bytes 11145216 | tf_op jit(solution)/shard_map/dot_general | solution.py:69
  129.5 4.3 %fusion.3 = f32[64,128,128]{2,1,0:T(8,128)} fusion(bf16[64,128,512]{2,1,0:T(8,128)(2,1)S(1)} %bitcast.45, bf16[512,128,1]{1,0,2:T(8,128)(2,1)S(1)} %bitcast.51), kind=kOutput, calls=%fused_computation.17 | convolution fusion | flops 1073741824 | bytes 12713984 | tf_op jit(solution)/shard_map/dot_general | solution.py:32
  133.8 10.5 %all-to-all-start.3 = ((f32[64,128,128]{2,1,0:T(8,128)}), f32[64,128,128]{2,1,0:T(8,128)}, u32[]{:S(2)}, u32[]{:S(2)}) async-start(f32[64,128,128]{2,1,0:T(8,128)} %fusion.3), calls=%async_computation.3 | async-start | bytes 8388608 | tf_op jit(solution)/shard_map/all_to_all | solution.py:54
  144.3 0.2 multiply_reduce_fusion.2
  144.5 4.8 %multiply_convert_fusion = bf16[512,8192]{1,0:T(8,128)(2,1)S(1)} fusion(bf16[512,8192]{1,0:T(8,128)(2,1)} %divide_convert_fusion, bf16[512,128]{1,0:T(8,128)(2,1)S(1)} %bitcast.52, bf16[8192,128]{1,0:T(8,128)(2,1)S(1)} %bitcast.48, f32[512]{0:T(512)S(1)} %multiply_reduce_fusion.2), kind=kOutput, calls=%fused_computation | convolution fusion | flops 1090519040 | bytes 19007488 | tf_op jit(solution)/shard_map/dot_general | solution.py:38
  149.3 2.4 convolution_multiply_fusion
  151.7 0.8 copy-done
  152.5 2.4 pad_maximum_fusion
  154.9 82.6 %all-to-all-done.3 = f32[64,128,128]{2,1,0:T(8,128)} async-done(((f32[64,128,128]{2,1,0:T(8,128)}), f32[64,128,128]{2,1,0:T(8,128)}, u32[]{:S(2)}, u32[]{:S(2)}) %all-to-all-start.3) | async-done | bytes 4194336 | tf_op jit(solution)/shard_map/all_to_all | solution.py:54
  237.5 7.5 %all-to-all-start.2 = ((f32[64,132,128]{2,1,0:T(8,128)}), f32[64,132,128]{2,1,0:T(8,128)}, u32[]{:S(2)}, u32[]{:S(2)}) async-start(f32[64,132,128]{2,1,0:T(8,128)} %pad_maximum_fusion), calls=%async_computation.2 | async-start | bytes 8912896 | tf_op jit(solution)/shard_map/all_to_all | solution.py:54
  245.0 0.2 copy.36
  245.3 5.7 %fusion.1 = bf16[512,128]{1,0:T(8,128)(2,1)S(1)} fusion(bf16[512,8192]{1,0:T(8,128)(2,1)} %copy-done, bf16[8192,128]{1,0:T(8,128)(2,1)S(1)} %bitcast.50), kind=kOutput, calls=%fused_computation.8 | convolution fusion | flops 1073872896 | bytes 10616832 | tf_op jit(solution)/shard_map/dot_general | solution.py:81
  251.1 0.7 convert_element_type.79
  251.9 0.7 multiply_convert_fusion.2
  252.5 3.0 reduce_sum.58
  255.6 88.0 %all-to-all-done.2 = f32[64,132,128]{2,1,0:T(8,128)} async-done(((f32[64,132,128]{2,1,0:T(8,128)}), f32[64,132,128]{2,1,0:T(8,128)}, u32[]{:S(2)}, u32[]{:S(2)}) %all-to-all-start.2) | async-done | bytes 4325408 | tf_op jit(solution)/shard_map/all_to_all | solution.py:54
  343.6 2.5 reduce_sum.57
  346.1 0.6 broadcast_in_dim.20
  346.7 15.3 %all-to-all-start.4 = ((f32[8,4,128]{2,1,0:T(4,128)}), f32[8,4,128]{2,1,0:T(4,128)S(1)}, u32[]{:S(2)}, u32[]{:S(2)}) async-start(f32[8,4,128]{2,1,0:T(4,128)} %broadcast_in_dim.20), calls=%async_computation.4 | async-start | bytes 32768 | tf_op jit(solution)/shard_map/all_to_all | solution.py:89
  362.0 0.6 fusion.2
  362.6 11.3 %all-to-all-done.4 = f32[8,4,128]{2,1,0:T(4,128)S(1)} async-done(((f32[8,4,128]{2,1,0:T(4,128)}), f32[8,4,128]{2,1,0:T(4,128)S(1)}, u32[]{:S(2)}, u32[]{:S(2)}) %all-to-all-start.4) | async-done | bytes 16416 | tf_op jit(solution)/shard_map/all_to_all | solution.py:89
  373.9 0.6 multiply_bitcast_fusion
  (19 shorter events, 0.5 us)
Async XLA Ops:
  0.6 72.2 %copy-start.3 = (bf16[1,128,512]{2,1,0:T(8,128)(2,1)S(1)}, bf16[1,128,512]{2,1,0:T(8,128)(2,1)}, u32[]{:S(2)}) copy-start(bf16[1,128,512]{2,1,0:T(8,128)(2,1)} %param.9) | copy-start | bytes 393220
  0.6 72.3 %copy-start.4 = (bf16[1,128,512]{2,1,0:T(8,128)(2,1)S(1)}, bf16[1,128,512]{2,1,0:T(8,128)(2,1)}, u32[]{:S(2)}) copy-start(bf16[1,128,512]{2,1,0:T(8,128)(2,1)} %param.5) | copy-start | bytes 393220
  66.1 57.5 %all-to-all-start.1 = ((bf16[64,128,128]{2,1,0:T(8,128)(2,1)}), bf16[64,128,128]{2,1,0:T(8,128)(2,1)S(1)}, u32[]{:S(2)}, u32[]{:S(2)}) async-start(bf16[64,128,128]{2,1,0:T(8,128)(2,1)} %broadcast_in_dim.17), calls=%async_computation.1 | async-start | bytes 4194304 | tf_op jit(solution)/shard_map/all_to_all | solution.py:44
  113.5 10.2 %copy-start.5 = (f32[512]{0:T(512)S(1)}, f32[512]{0:T(512)}, u32[]{:S(2)}) copy-start(f32[512]{0:T(512)} %param.8) | copy-start | bytes 6148
  123.6 5.9 %copy-start.1 = (bf16[8192,512]{1,0:T(8,128)(2,1)S(1)}, bf16[8192,512]{1,0:T(8,128)(2,1)}, u32[]{:S(2)}) copy-start(bf16[8192,512]{1,0:T(8,128)(2,1)} %copy.42) | copy-start | bytes 25165828
  133.8 103.7 %all-to-all-start.3 = ((f32[64,128,128]{2,1,0:T(8,128)}), f32[64,128,128]{2,1,0:T(8,128)}, u32[]{:S(2)}, u32[]{:S(2)}) async-start(f32[64,128,128]{2,1,0:T(8,128)} %fusion.3), calls=%async_computation.3 | async-start | bytes 8388608 | tf_op jit(solution)/shard_map/all_to_all | solution.py:54
  149.3 3.2 copy-start
  152.5 92.8 %copy-start.2 = (bf16[64,128,128]{2,1,0:T(8,128)(2,1)S(1)}, bf16[64,128,128]{2,1,0:T(8,128)(2,1)}, u32[]{:S(2)}) copy-start(bf16[64,128,128]{2,1,0:T(8,128)(2,1)} %all_to_all.25) | copy-start | bytes 6291460
  237.5 106.1 %all-to-all-start.2 = ((f32[64,132,128]{2,1,0:T(8,128)}), f32[64,132,128]{2,1,0:T(8,128)}, u32[]{:S(2)}, u32[]{:S(2)}) async-start(f32[64,132,128]{2,1,0:T(8,128)} %pad_maximum_fusion), calls=%async_computation.2 | async-start | bytes 8912896 | tf_op jit(solution)/shard_map/all_to_all | solution.py:54
  346.7 27.2 %all-to-all-start.4 = ((f32[8,4,128]{2,1,0:T(4,128)}), f32[8,4,128]{2,1,0:T(4,128)S(1)}, u32[]{:S(2)}, u32[]{:S(2)}) async-start(f32[8,4,128]{2,1,0:T(4,128)} %broadcast_in_dim.20), calls=%async_computation.4 | async-start | bytes 32768 | tf_op jit(solution)/shard_map/all_to_all | solution.py:89

commit v5 on v4

--- a/solution.py
+++ b/solution.py
@@ -51,7 +51,8 @@
 
 
 def reduce_seq(terms):
-    return jnp.sum(lax.all_to_all(terms, "seq", split_axis=0, concat_axis=0, tiled=True), axis=0)
+    recv = lax.all_to_all(terms, "seq", split_axis=0, concat_axis=0, tiled=True)
+    return jnp.sum(recv.astype(jnp.float32), axis=0)
 
 
 def body(query, key_in, value_in, out_gain, cotangent):
@@ -74,17 +75,26 @@
     grad_out = (upstream * out_gain).astype(jnp.bfloat16)
     grad_rows = to_rows(grad_out, HEADS)
     delta_rows = jnp.sum(grad_rows.astype(jnp.float32) * out_rows, axis=1, keepdims=True)
-    value_terms = contract_first(weights, grad_rows).reshape(shards, positions, VAL)
+    value_terms = contract_first(weights, grad_rows).reshape(shards, positions, VAL).astype(jnp.bfloat16)
     grad_value = reduce_seq(value_terms)
     d_prob = contract_last(grad_rows, value_mat)
     d_score = (weights.astype(jnp.float32) * (d_prob - delta_rows)).astype(jnp.bfloat16)
     query_acc = jnp.dot(d_score, key_mat, preferred_element_type=jnp.float32)
     key_terms = (contract_first(d_score, query_rows) * score_scale).reshape(shards, positions, KEY)
+    gain_high = gain_rows.astype(jnp.bfloat16)
+    gain_low = (gain_rows - gain_high.astype(jnp.float32)).astype(jnp.bfloat16)
+    gain_pair = jnp.concatenate([gain_high, gain_low], axis=0)
     key_recv = reduce_seq(
-        jnp.concatenate([key_terms, jnp.broadcast_to(gain_rows[None], (shards, HEADS, KEY))], axis=1)
+        jnp.concatenate(
+            [
+                key_terms.astype(jnp.bfloat16),
+                jnp.broadcast_to(gain_pair[None], (shards, 2 * HEADS, KEY)),
+            ],
+            axis=1,
+        )
     )
     grad_key = key_recv[:positions]
-    gain_seq = key_recv[positions:]
+    gain_seq = key_recv[positions : positions + HEADS] + key_recv[positions + HEADS :]
     gain_total = jnp.sum(
         lax.all_to_all(
             jnp.broadcast_to(gain_seq[None], (groups,) + gain_seq.shape),

time: 375 us -> 280 us (0.75)
  waiting for transfers between devices: 182 us -> 88.9 us
    all_to_all x2, waiting for transfers between devices: 171 us -> 77.7 us  [reduce_seq(): recv = lax.all_to_all(terms, 'seq', split_axis=0, concat_axis=0, tiled=True)]
  transfers between devices with their start and end apart: 4 -> 4, of which waited for: 3 -> 3; matrix products, arithmetic and copies ran while one was open for 19% -> 25% of each run, Pallas kernels for 0% -> 0%
where the time goes in v5:
time: 280 us; the launch traced here: 279 us
  waiting for transfers between devices  88.9 us (32%)
  blocking collectives  61.6 us (22%)
  starting transfers between devices  38.4 us (14%)
  other arithmetic  34.8 us (12%)
  matrix products  32.7 us (12%)
  local copies, waits for them, and re-layouts  21.7 us (8%)
    all_to_all x2, waiting for transfers between devices, reduce_seq(): recv = lax.all_to_all(terms, 'seq', split_axis=0, concat_axis=0, tiled=True)  77.7 us
    all_to_all x1, blocking collectives, gather_seq(): lax.all_to_all(jnp.broadcast_to(local[None], (shards,) + local.shape), 's...  61.6 us
    all_to_all x2, starting transfers between devices, reduce_seq(): recv = lax.all_to_all(terms, 'seq', split_axis=0, concat_axis=0, tiled=True)  16.7 us
    all_to_all x1, starting transfers between devices, body(): lax.all_to_all(jnp.broadcast_to(gain_seq[None], (groups,) + gain_seq.shap...  15.1 us
    dot_general x2, matrix products, contract_last(): lax.dot_general(left_mat, right_mat, (((1,), (1,)), ((), ())), preferred_...  14.4 us
    dot_general x1, local copies, waits for them, and re-layouts, contract_first(): lax.dot_general(left_mat, right_mat, (((0,), (0,)), ((), ())), preferred_...  11.9 us
    all_to_all x1, waiting for transfers between devices, body(): lax.all_to_all(jnp.broadcast_to(gain_seq[None], (groups,) + gain_seq.shap...  11.3 us
    convert_element_type x1, other arithmetic, body(): (expo_rows / jnp.sum(expo_rows, axis=1, keepdims=True)).astype(jnp.bfloat16)  10.1 us
  transfers between devices with their start and end apart: 4, of which 3 were waited for; matrix products, arithmetic and copies ran while one was open for 25% of the time, Pallas kernels for 0%

profile of v5, /device:TPU:1, one launch (start us, length us, event | category | flops | bytes accessed | tf_op | source)
XLA Modules:
  0.0 278.9 jit_solution(16818471608540708308)
XLA Ops:
  0.7 1.3 broadcast_in_dim.17
  2.0 61.6 %all_to_all.25 = bf16[64,128,128]{2,1,0:T(8,128)(2,1)} all-to-all(bf16[64,128,128]{2,1,0:T(8,128)(2,1)S(1)} %broadcast_in_dim.17), channel_id=1, replica_groups=mesh['dp'=8,'seq'=64] {'seq'}, dimensions={0} | all-to-all | bytes 4194304 | tf_op jit(solution)/shard_map/all_to_all | solution.py:44
  63.5 2.6 broadcast_in_dim.19
  66.1 6.6 %all-to-all-start.1 = ((bf16[64,128,128]{2,1,0:T(8,128)(2,1)}), bf16[64,128,128]{2,1,0:T(8,128)(2,1)S(1)}, u32[]{:S(2)}, u32[]{:S(2)}) async-start(bf16[64,128,128]{2,1,0:T(8,128)(2,1)} %broadcast_in_dim.19), calls=%async_computation.1 | async-start | bytes 4194304 | tf_op jit(solution)/shard_map/all_to_all | solution.py:44
  73.0 0.1 copy.35
  73.2 9.6 %multiply_reduce_fusion = (f32[512]{0:T(512)S(1)}, f32[512,8192]{1,0:T(8,128)}) fusion(bf16[512,128]{1,0:T(8,128)(2,1)S(1)} %bitcast.52, bf16[8192,128]{1,0:T(8,128)(2,1)} %bitcast.47), kind=kOutput, calls=%fused_computation.3 | convolution fusion | flops 1082129920 | bytes 19007488 | tf_op jit(solution)/shard_map/dot_general | solution.py:38
  82.8 8.6 %fusion = f32[512]{0:T(512)S(1)} fusion(f32[512,8192]{1,0:T(8,128)} %get-tuple-element.10, f32[512]{0:T(512)S(1)} %get-tuple-element.9), kind=kLoop, calls=%fused_computation.4 | loop fusion | flops 12582400 | bytes 16781312 | tf_op jit(solution)/shard_map/reduce_sum | solution.py:69
  91.4 10.1 %fusion.16 = bf16[8192,512]{0,1:T(8,128)(2,1)} fusion(f32[512]{0:T(512)S(1)} %fusion, f32[512]{0:T(512)S(1)} %get-tuple-element.9, f32[512,8192]{1,0:T(8,128)} %get-tuple-element.10), kind=kLoop, calls=%fused_computation.22 | loop fusion | flops 16777216 | bytes 25169920 | tf_op jit(solution)/shard_map/div | solution.py:69
  101.6 11.9 %copy.42 = bf16[8192,512]{1,0:T(8,128)(2,1)} copy(bf16[8192,512]{0,1:T(8,128)(2,1)} %fusion.16) | data formatting | bytes 16777216 | tf_op jit(solution)/shard_map/dot_general | solution.py:32
  113.5 10.1 %divide_convert_fusion = bf16[512,8192]{1,0:T(8,128)(2,1)} fusion(f32[512,8192]{1,0:T(8,128)} %get-tuple-element.10, f32[512]{0:T(512)S(1)} %fusion, f32[512]{0:T(512)S(1)} %get-tuple-element.9), kind=kLoop, calls=%fused_computation.1 | loop fusion | flops 16777216 | bytes 25169920 | tf_op jit(solution)/shard_map/convert_element_type | solution.py:69
  123.6 5.9 %multiply_reduce_fusion.1 = (f32[4,128]{1,0:T(4,128)S(1)}, bf16[128,4,128]{2,0,1:T(8,128)(2,1)S(1)}, f32[512,128]{1,0:T(8,128)S(1)}) fusion(f32[128,4,128]{2,1,0:T(4,128)S(1)} %reshape.107, f32[4,128]{1,0:T(4,128)S(1)} %bitcast.59, bf16[512,8192]{1,0:T(8,128)(2,1)} %divide_convert_fusion, bf16[8192,128]{1,0:T(8,128)(2,1)S(1)} %bitcast.44), kind=kOutput, calls=%fused_computation.12 | convolution fusion | flops 1074003456 | bytes 11145216 | tf_op jit(solution)/shard_map/dot_general | solution.py:70
  129.5 3.7 %convolution_convert_fusion = bf16[64,128,128]{2,1,0:T(8,128)(2,1)} fusion(bf16[64,128,512]{2,1,0:T(8,128)(2,1)S(1)} %bitcast.43, bf16[512,128,1]{1,0,2:T(8,128)(2,1)S(1)} %bitcast.49), kind=kOutput, calls=%fused_computation.9 | convolution fusion | flops 1074790400 | bytes 10616832 | tf_op jit(solution)/shard_map/dot_general | solution.py:32
  133.2 10.5 %all-to-all-start.3 = ((bf16[64,128,128]{2,1,0:T(8,128)(2,1)}), bf16[64,128,128]{2,1,0:T(8,128)(2,1)}, u32[]{:S(2)}, u32[]{:S(2)}) async-start(bf16[64,128,128]{2,1,0:T(8,128)(2,1)} %convolution_convert_fusion), calls=%async_computation.3 | async-start | bytes 4194304 | tf_op jit(solution)/shard_map/all_to_all | solution.py:54
  143.7 0.2 multiply_reduce_fusion.2
  143.9 4.8 %multiply_convert_fusion = bf16[512,8192]{1,0:T(8,128)(2,1)S(1)} fusion(bf16[512,8192]{1,0:T(8,128)(2,1)} %divide_convert_fusion, bf16[512,128]{1,0:T(8,128)(2,1)S(1)} %bitcast.50, bf16[8192,128]{1,0:T(8,128)(2,1)S(1)} %bitcast.45, f32[512]{0:T(512)S(1)} %multiply_reduce_fusion.2), kind=kOutput, calls=%fused_computation | convolution fusion | flops 1090519040 | bytes 19007488 | tf_op jit(solution)/shard_map/dot_general | solution.py:38
  148.7 3.2 %copy-done.1 = bf16[512,8192]{1,0:T(8,128)(2,1)} copy-done((bf16[512,8192]{1,0:T(8,128)(2,1)}, bf16[512,8192]{1,0:T(8,128)(2,1)S(1)}, u32[]{:S(2)}) %copy-start.1) | copy-done | bytes 8388632
  151.9 2.4 fusion.1
  154.3 1.6 pad_maximum_fusion
  155.9 36.7 %all-to-all-done.3 = bf16[64,128,128]{2,1,0:T(8,128)(2,1)} async-done(((bf16[64,128,128]{2,1,0:T(8,128)(2,1)}), bf16[64,128,128]{2,1,0:T(8,128)(2,1)}, u32[]{:S(2)}, u32[]{:S(2)}) %all-to-all-start.3) | async-done | bytes 2097184 | tf_op jit(solution)/shard_map/all_to_all | solution.py:54
  192.6 6.2 %all-to-all-start.2 = ((bf16[64,136,128]{2,1,0:T(8,128)(2,1)}), bf16[64,136,128]{2,1,0:T(8,128)(2,1)S(1)}, u32[]{:S(2)}, u32[]{:S(2)}) async-start(bf16[64,136,128]{2,1,0:T(8,128)(2,1)} %pad_maximum_fusion), calls=%async_computation.2 | async-start | bytes 4456448 | tf_op jit(solution)/shard_map/all_to_all | solution.py:54
  198.8 0.2 copy.36
  199.1 6.3 %fusion.2 = bf16[512,128]{1,0:T(8,128)(2,1)S(1)} fusion(bf16[512,8192]{1,0:T(8,128)(2,1)} %copy-done.1, bf16[8192,128]{1,0:T(8,128)(2,1)} %bitcast.48), kind=kOutput, calls=%fused_computation.11 | convolution fusion | flops 1073872896 | bytes 10616832 | tf_op jit(solution)/shard_map/dot_general | solution.py:82
  205.5 0.7 convert_element_type.89
  206.2 0.7 multiply_convert_fusion.2
  206.9 2.5 reduce_sum.61
  209.4 41.0 %all-to-all-done.2 = bf16[64,136,128]{2,1,0:T(8,128)(2,1)S(1)} async-done(((bf16[64,136,128]{2,1,0:T(8,128)(2,1)}), bf16[64,136,128]{2,1,0:T(8,128)(2,1)S(1)}, u32[]{:S(2)}, u32[]{:S(2)}) %all-to-all-start.2) | async-done | bytes 2228256 | tf_op jit(solution)/shard_map/all_to_all | solution.py:54
  250.4 0.3 convert_reduce_fusion
  250.8 0.6 broadcast_in_dim.46
  251.4 15.1 %all-to-all-start.4 = ((f32[8,4,128]{2,1,0:T(4,128)}), f32[8,4,128]{2,1,0:T(4,128)S(1)}, u32[]{:S(2)}, u32[]{:S(2)}) async-start(f32[8,4,128]{2,1,0:T(4,128)} %broadcast_in_dim.46), calls=%async_computation.4 | async-start | bytes 32768 | tf_op jit(solution)/shard_map/all_to_all | solution.py:99
  266.5 0.6 fusion.3
  267.1 11.3 %all-to-all-done.4 = f32[8,4,128]{2,1,0:T(4,128)S(1)} async-done(((f32[8,4,128]{2,1,0:T(4,128)}), f32[8,4,128]{2,1,0:T(4,128)S(1)}, u32[]{:S(2)}, u32[]{:S(2)}) %all-to-all-start.4) | async-done | bytes 16416 | tf_op jit(solution)/shard_map/all_to_all | solution.py:99
  278.3 0.6 multiply_bitcast_fusion
  (19 shorter events, 0.5 us)
Async XLA Ops:
  0.6 72.2 %copy-start.2 = (bf16[1,128,512]{2,1,0:T(8,128)(2,1)S(1)}, bf16[1,128,512]{2,1,0:T(8,128)(2,1)}, u32[]{:S(2)}) copy-start(bf16[1,128,512]{2,1,0:T(8,128)(2,1)} %param.9) | copy-start | bytes 393220
  0.6 72.3 %copy-start.3 = (bf16[1,128,512]{2,1,0:T(8,128)(2,1)S(1)}, bf16[1,128,512]{2,1,0:T(8,128)(2,1)}, u32[]{:S(2)}) copy-start(bf16[1,128,512]{2,1,0:T(8,128)(2,1)} %param.5) | copy-start | bytes 393220
  66.1 57.5 %all-to-all-start.1 = ((bf16[64,128,128]{2,1,0:T(8,128)(2,1)}), bf16[64,128,128]{2,1,0:T(8,128)(2,1)S(1)}, u32[]{:S(2)}, u32[]{:S(2)}) async-start(bf16[64,128,128]{2,1,0:T(8,128)(2,1)} %broadcast_in_dim.19), calls=%async_computation.1 | async-start | bytes 4194304 | tf_op jit(solution)/shard_map/all_to_all | solution.py:44
  113.5 10.2 %copy-start.4 = (f32[512]{0:T(512)S(1)}, f32[512]{0:T(512)}, u32[]{:S(2)}) copy-start(f32[512]{0:T(512)} %param.8) | copy-start | bytes 6148
  123.6 5.9 %copy-start = (bf16[8192,512]{1,0:T(8,128)(2,1)S(1)}, bf16[8192,512]{1,0:T(8,128)(2,1)}, u32[]{:S(2)}) copy-start(bf16[8192,512]{1,0:T(8,128)(2,1)} %copy.42) | copy-start | bytes 25165828
  133.2 59.4 %all-to-all-start.3 = ((bf16[64,128,128]{2,1,0:T(8,128)(2,1)}), bf16[64,128,128]{2,1,0:T(8,128)(2,1)}, u32[]{:S(2)}, u32[]{:S(2)}) async-start(bf16[64,128,128]{2,1,0:T(8,128)(2,1)} %convolution_convert_fusion), calls=%async_computation.3 | async-start | bytes 4194304 | tf_op jit(solution)/shard_map/all_to_all | solution.py:54
  148.7 3.2 %copy-start.1 = (bf16[512,8192]{1,0:T(8,128)(2,1)}, bf16[512,8192]{1,0:T(8,128)(2,1)S(1)}, u32[]{:S(2)}) copy-start(bf16[512,8192]{1,0:T(8,128)(2,1)S(1)} %multiply_convert_fusion) | copy-start | bytes 25165828
  192.6 57.8 %all-to-all-start.2 = ((bf16[64,136,128]{2,1,0:T(8,128)(2,1)}), bf16[64,136,128]{2,1,0:T(8,128)(2,1)S(1)}, u32[]{:S(2)}, u32[]{:S(2)}) async-start(bf16[64,136,128]{2,1,0:T(8,128)(2,1)} %pad_maximum_fusion), calls=%async_computation.2 | async-start | bytes 4456448 | tf_op jit(solution)/shard_map/all_to_all | solution.py:54
  251.4 27.0 %all-to-all-start.4 = ((f32[8,4,128]{2,1,0:T(4,128)}), f32[8,4,128]{2,1,0:T(4,128)S(1)}, u32[]{:S(2)}, u32[]{:S(2)}) async-start(f32[8,4,128]{2,1,0:T(4,128)} %broadcast_in_dim.46), calls=%async_computation.4 | async-start | bytes 32768 | tf_op jit(solution)/shard_map/all_to_all | solution.py:99

commit v6 on v5

--- a/solution.py
+++ b/solution.py
@@ -81,6 +81,7 @@
     d_score = (weights.astype(jnp.float32) * (d_prob - delta_rows)).astype(jnp.bfloat16)
     query_acc = jnp.dot(d_score, key_mat, preferred_element_type=jnp.float32)
     key_terms = (contract_first(d_score, query_rows) * score_scale).reshape(shards, positions, KEY)
+    gain_rows = lax.psum(gain_rows, "dp")
     gain_high = gain_rows.astype(jnp.bfloat16)
     gain_low = (gain_rows - gain_high.astype(jnp.float32)).astype(jnp.bfloat16)
     gain_pair = jnp.concatenate([gain_high, gain_low], axis=0)
@@ -95,16 +96,7 @@
     )
     grad_key = key_recv[:positions]
     gain_seq = key_recv[positions : positions + HEADS] + key_recv[positions + HEADS :]
-    gain_total = jnp.sum(
-        lax.all_to_all(
-            jnp.broadcast_to(gain_seq[None], (groups,) + gain_seq.shape),
-            "dp",
-            split_axis=0,
-            concat_axis=0,
-            tiled=True,
-        ),
-        axis=0,
-    ).reshape(HEADS * VAL)
+    gain_total = gain_seq.reshape(HEADS * VAL)
     grad_gain = gain_total / math.sqrt(groups * shards * positions)
     grad_query = to_tokens(query_acc * score_scale, HEADS).astype(jnp.bfloat16)
     return (

time: 280 us -> 282 us (level)
  blocking collectives: 61.6 us -> 112 us
  waiting for transfers between devices: 88.9 us -> 41 us
    psum x0 -> x1, blocking collectives: none -> 50 us  [body(): gain_rows = lax.psum(gain_rows, 'dp')]
    all_to_all x2, waiting for transfers between devices: 77.7 us -> 41 us  [reduce_seq(): recv = lax.all_to_all(terms, 'seq', split_axis=0, concat_axis=0, tiled=True)]
    all_to_all x1 -> x0, starting transfers between devices: 15.1 us -> none  [body(): lax.all_to_all(jnp.broadcast_to(gain_seq[None], (groups,) + gain_seq.shap...]
    all_to_all x2, starting transfers between devices: 16.7 us -> 31.7 us  [reduce_seq(): recv = lax.all_to_all(terms, 'seq', split_axis=0, concat_axis=0, tiled=True)]
    all_to_all x1 -> x0, waiting for transfers between devices: 11.3 us -> none  [body(): lax.all_to_all(jnp.broadcast_to(gain_seq[None], (groups,) + gain_seq.shap...]
  transfers between devices with their start and end apart: 4 -> 3, of which waited for: 3 -> 1; matrix products, arithmetic and copies ran while one was open for 25% -> 25% of each run, Pallas kernels for 0% -> 0%
where the time goes in v6:
time: 282 us; the launch traced here: 280 us
  blocking collectives  112 us (40%)
  waiting for transfers between devices  41 us (15%)
  starting transfers between devices  38.3 us (14%)
  other arithmetic  34.8 us (12%)
  matrix products  32.7 us (12%)
  local copies, waits for them, and re-layouts  21.1 us (7%)
    all_to_all x1, blocking collectives, gather_seq(): lax.all_to_all(jnp.broadcast_to(local[None], (shards,) + local.shape), 's...  61.6 us
    psum x1, blocking collectives, body(): gain_rows = lax.psum(gain_rows, 'dp')  50 us
    all_to_all x2, waiting for transfers between devices, reduce_seq(): recv = lax.all_to_all(terms, 'seq', split_axis=0, concat_axis=0, tiled=True)  41 us
    all_to_all x2, starting transfers between devices, reduce_seq(): recv = lax.all_to_all(terms, 'seq', split_axis=0, concat_axis=0, tiled=True)  31.7 us
    dot_general x2, matrix products, contract_last(): lax.dot_general(left_mat, right_mat, (((1,), (1,)), ((), ())), preferred_...  14.4 us
    dot_general x1, local copies, waits for them, and re-layouts, contract_first(): lax.dot_general(left_mat, right_mat, (((0,), (0,)), ((), ())), preferred_...  11.9 us
    convert_element_type x1, other arithmetic, body(): (expo_rows / jnp.sum(expo_rows, axis=1, keepdims=True)).astype(jnp.bfloat16)  10.1 us
    div x1, other arithmetic, body(): expo_rows / jnp.sum(expo_rows, axis=1, keepdims=True)  10.1 us
  transfers between devices with their start and end apart: 3, of which 1 were waited for; matrix products, arithmetic and copies ran while one was open for 25% of the time, Pallas kernels for 0%

profile of v6, /device:TPU:1, one launch (start us, length us, event | category | flops | bytes accessed | tf_op | source)
XLA Modules:
  0.0 280.3 jit_solution(6249376349930338529)
XLA Ops:
  0.7 1.3 broadcast_in_dim.15
  2.0 61.6 %all_to_all.20 = bf16[64,128,128]{2,1,0:T(8,128)(2,1)} all-to-all(bf16[64,128,128]{2,1,0:T(8,128)(2,1)S(1)} %broadcast_in_dim.15), channel_id=1, replica_groups=mesh['dp'=8,'seq'=64] {'seq'}, dimensions={0} | all-to-all | bytes 4194304 | tf_op jit(solution)/shard_map/all_to_all | solution.py:44
  63.5 2.6 broadcast_in_dim.17
  66.1 6.6 %all-to-all-start.1 = ((bf16[64,128,128]{2,1,0:T(8,128)(2,1)}), bf16[64,128,128]{2,1,0:T(8,128)(2,1)S(1)}, u32[]{:S(2)}, u32[]{:S(2)}) async-start(bf16[64,128,128]{2,1,0:T(8,128)(2,1)} %broadcast_in_dim.17), calls=%async_computation.1 | async-start | bytes 4194304 | tf_op jit(solution)/shard_map/all_to_all | solution.py:44
  72.9 0.1 copy.20
  73.0 0.1 copy.21
  73.2 9.6 %multiply_reduce_fusion = (f32[512]{0:T(512)S(1)}, f32[512,8192]{1,0:T(8,128)}) fusion(bf16[512,128]{1,0:T(8,128)(2,1)S(1)} %bitcast.52, bf16[8192,128]{1,0:T(8,128)(2,1)} %bitcast.47), kind=kOutput, calls=%fused_computation.3 | convolution fusion | flops 1082129920 | bytes 19007488 | tf_op jit(solution)/shard_map/dot_general | solution.py:38
  82.8 8.6 %fusion = f32[512]{0:T(512)S(1)} fusion(f32[512,8192]{1,0:T(8,128)} %get-tuple-element.10, f32[512]{0:T(512)S(1)} %get-tuple-element.9), kind=kLoop, calls=%fused_computation.4 | loop fusion | flops 12582400 | bytes 16781312 | tf_op jit(solution)/shard_map/reduce_sum | solution.py:69
  91.4 10.1 %fusion.18 = bf16[8192,512]{0,1:T(8,128)(2,1)} fusion(f32[512]{0:T(512)S(1)} %fusion, f32[512]{0:T(512)S(1)} %get-tuple-element.9, f32[512,8192]{1,0:T(8,128)} %get-tuple-element.10), kind=kLoop, calls=%fused_computation.23 | loop fusion | flops 16777216 | bytes 25169920 | tf_op jit(solution)/shard_map/div | solution.py:69
  101.6 11.9 %copy.27 = bf16[8192,512]{1,0:T(8,128)(2,1)} copy(bf16[8192,512]{0,1:T(8,128)(2,1)} %fusion.18) | data formatting | bytes 16777216 | tf_op jit(solution)/shard_map/dot_general | solution.py:32
  113.5 10.1 %divide_convert_fusion = bf16[512,8192]{1,0:T(8,128)(2,1)} fusion(f32[512,8192]{1,0:T(8,128)} %get-tuple-element.10, f32[512]{0:T(512)S(1)} %fusion, f32[512]{0:T(512)S(1)} %get-tuple-element.9), kind=kLoop, calls=%fused_computation.1 | loop fusion | flops 16777216 | bytes 25169920 | tf_op jit(solution)/shard_map/convert_element_type | solution.py:69
  123.6 5.9 %multiply_reduce_fusion.1 = (f32[4,128]{1,0:T(4,128)S(1)}, bf16[128,4,128]{2,0,1:T(8,128)(2,1)S(1)}, f32[512,128]{1,0:T(8,128)S(1)}) fusion(f32[128,4,128]{2,1,0:T(4,128)S(1)} %reshape.106, f32[4,128]{1,0:T(4,128)S(1)} %bitcast.59, bf16[512,8192]{1,0:T(8,128)(2,1)} %divide_convert_fusion, bf16[8192,128]{1,0:T(8,128)(2,1)S(1)} %bitcast.44), kind=kOutput, calls=%fused_computation.12 | convolution fusion | flops 1074003456 | bytes 11145216 | tf_op jit(solution)/shard_map/dot_general | solution.py:70
  129.5 3.7 %convolution_convert_fusion = bf16[64,128,128]{2,1,0:T(8,128)(2,1)} fusion(bf16[64,128,512]{2,1,0:T(8,128)(2,1)S(1)} %bitcast.43, bf16[512,128,1]{1,0,2:T(8,128)(2,1)S(1)} %bitcast.49), kind=kOutput, calls=%fused_computation.9 | convolution fusion | flops 1074790400 | bytes 10616832 | tf_op jit(solution)/shard_map/dot_general | solution.py:32
  133.2 10.5 %all-to-all-start.3 = ((bf16[64,128,128]{2,1,0:T(8,128)(2,1)}), bf16[64,128,128]{2,1,0:T(8,128)(2,1)}, u32[]{:S(2)}, u32[]{:S(2)}) async-start(bf16[64,128,128]{2,1,0:T(8,128)(2,1)} %convolution_convert_fusion), calls=%async_computation.3 | async-start | bytes 4194304 | tf_op jit(solution)/shard_map/all_to_all | solution.py:54
  143.7 50.0 %psum.7 = f32[4,128]{1,0:T(4,128)S(1)} all-reduce(f32[4,128]{1,0:T(4,128)S(1)} %get-tuple-element.7), channel_id=1, replica_groups=mesh['dp'=8,'seq'=64] {'dp'}, use_global_device_ids=true, to_apply=%region_4.0 | all-reduce | flops 512 | bytes 4096 | tf_op jit(solution)/shard_map/psum | solution.py:84
  193.7 0.2 multiply_reduce_fusion.2
  193.9 4.8 %multiply_convert_fusion = bf16[512,8192]{1,0:T(8,128)(2,1)S(1)} fusion(bf16[512,8192]{1,0:T(8,128)(2,1)} %divide_convert_fusion, bf16[512,128]{1,0:T(8,128)(2,1)S(1)} %bitcast.50, bf16[8192,128]{1,0:T(8,128)(2,1)S(1)} %bitcast.45, f32[512]{0:T(512)S(1)} %multiply_reduce_fusion.2), kind=kOutput, calls=%fused_computation | convolution fusion | flops 1090519040 | bytes 19007488 | tf_op jit(solution)/shard_map/dot_general | solution.py:38
  198.7 3.2 %copy-done.1 = bf16[512,8192]{1,0:T(8,128)(2,1)} copy-done((bf16[512,8192]{1,0:T(8,128)(2,1)}, bf16[512,8192]{1,0:T(8,128)(2,1)S(1)}, u32[]{:S(2)}) %copy-start.1) | copy-done | bytes 8388632
  201.9 2.4 fusion.1
  204.3 1.6 pad_maximum_fusion
  205.9 21.2 %all-to-all-start.2 = ((bf16[64,136,128]{2,1,0:T(8,128)(2,1)}), bf16[64,136,128]{2,1,0:T(8,128)(2,1)S(1)}, u32[]{:S(2)}, u32[]{:S(2)}) async-start(bf16[64,136,128]{2,1,0:T(8,128)(2,1)} %pad_maximum_fusion), calls=%async_computation.2 | async-start | bytes 4456448 | tf_op jit(solution)/shard_map/all_to_all | solution.py:54
  227.1 0.2 copy.22
  227.3 0.1 reshape.104
  227.4 6.3 %fusion.2 = bf16[512,128]{1,0:T(8,128)(2,1)S(1)} fusion(bf16[512,8192]{1,0:T(8,128)(2,1)} %copy-done.1, bf16[8192,128]{1,0:T(8,128)(2,1)} %bitcast.48), kind=kOutput, calls=%fused_computation.11 | convolution fusion | flops 1073872896 | bytes 10616832 | tf_op jit(solution)/shard_map/dot_general | solution.py:82
  233.7 0.1 copy.24
  233.8 0.7 convert_element_type.89
  234.5 0.7 multiply_convert_fusion.2
  235.2 2.5 reduce_sum.52
  237.7 41.0 %all-to-all-done.2 = bf16[64,136,128]{2,1,0:T(8,128)(2,1)S(1)} async-done(((bf16[64,136,128]{2,1,0:T(8,128)(2,1)}), bf16[64,136,128]{2,1,0:T(8,128)(2,1)S(1)}, u32[]{:S(2)}, u32[]{:S(2)}) %all-to-all-start.2) | async-done | bytes 2228256 | tf_op jit(solution)/shard_map/all_to_all | solution.py:54
  278.7 0.3 convert_reduce_fusion
  279.0 0.6 fusion.3
  279.7 0.6 fusion.5
  (15 shorter events, 0.1 us)
Async XLA Ops:
  0.6 72.2 %copy-start.2 = (bf16[1,128,512]{2,1,0:T(8,128)(2,1)S(1)}, bf16[1,128,512]{2,1,0:T(8,128)(2,1)}, u32[]{:S(2)}) copy-start(bf16[1,128,512]{2,1,0:T(8,128)(2,1)} %param.9) | copy-start | bytes 393220
  0.6 72.3 %copy-start.3 = (bf16[1,128,512]{2,1,0:T(8,128)(2,1)S(1)}, bf16[1,128,512]{2,1,0:T(8,128)(2,1)}, u32[]{:S(2)}) copy-start(bf16[1,128,512]{2,1,0:T(8,128)(2,1)} %param.5) | copy-start | bytes 393220
  66.1 57.5 %all-to-all-start.1 = ((bf16[64,128,128]{2,1,0:T(8,128)(2,1)}), bf16[64,128,128]{2,1,0:T(8,128)(2,1)S(1)}, u32[]{:S(2)}, u32[]{:S(2)}) async-start(bf16[64,128,128]{2,1,0:T(8,128)(2,1)} %broadcast_in_dim.17), calls=%async_computation.1 | async-start | bytes 4194304 | tf_op jit(solution)/shard_map/all_to_all | solution.py:44
  113.5 10.2 %copy-start.4 = (f32[512]{0:T(512)S(1)}, f32[512]{0:T(512)}, u32[]{:S(2)}) copy-start(f32[512]{0:T(512)} %param.8) | copy-start | bytes 6148
  123.6 5.9 %copy-start = (bf16[8192,512]{1,0:T(8,128)(2,1)S(1)}, bf16[8192,512]{1,0:T(8,128)(2,1)}, u32[]{:S(2)}) copy-start(bf16[8192,512]{1,0:T(8,128)(2,1)} %copy.27) | copy-start | bytes 25165828
  133.2 72.7 %all-to-all-start.3 = ((bf16[64,128,128]{2,1,0:T(8,128)(2,1)}), bf16[64,128,128]{2,1,0:T(8,128)(2,1)}, u32[]{:S(2)}, u32[]{:S(2)}) async-start(bf16[64,128,128]{2,1,0:T(8,128)(2,1)} %convolution_convert_fusion), calls=%async_computation.3 | async-start | bytes 4194304 | tf_op jit(solution)/shard_map/all_to_all | solution.py:54
  198.6 3.2 %copy-start.1 = (bf16[512,8192]{1,0:T(8,128)(2,1)}, bf16[512,8192]{1,0:T(8,128)(2,1)S(1)}, u32[]{:S(2)}) copy-start(bf16[512,8192]{1,0:T(8,128)(2,1)S(1)} %multiply_convert_fusion) | copy-start | bytes 25165828
  205.9 72.8 %all-to-all-start.2 = ((bf16[64,136,128]{2,1,0:T(8,128)(2,1)}), bf16[64,136,128]{2,1,0:T(8,128)(2,1)S(1)}, u32[]{:S(2)}, u32[]{:S(2)}) async-start(bf16[64,136,128]{2,1,0:T(8,128)(2,1)} %pad_maximum_fusion), calls=%async_computation.2 | async-start | bytes 4456448 | tf_op jit(solution)/shard_map/all_to_all | solution.py:54
